TPU v7x, 256 devices: a whole 4x4x8 slice. The times are simulated.
256 devices in a mesh: user: 16 (over z, core), item: 16 (over y, x).
Axes of the slice: x: 4, y: 4, z: 8, core: 2. Of those that a mesh axis runs over, the one named last changes fastest.
Arguments:
- ratings: bfloat16 [30720, 128, 128], P(('user', 'item')), may hold values from -6 to 6
- weights: bfloat16 [30720, 128, 128], P(('user', 'item')), may hold values from 0.19921875 to 2
- row_masks: int32 [30720, 4], P(('user', 'item')), may hold values from -2147483648 to 2147483646
- tile_users: int32 [30720], P(('user', 'item')), may hold values from 0 to 15
- tile_items: int32 [30720], P(('user', 'item')), may hold values from 0 to 15
- tile_counts: int32 [256], P(('user', 'item')), may hold values from 1 to 120
- users: float32 [32768, 128], P(('user', 'item')), may hold values from -1.8 to 1.8
- items: float32 [2048, 128], P('item'), may hold values from -1.8 to 1.8
Outputs:
- new_users: float32 [32768, 128], P(('user', 'item'))
- new_items: float32 [2048, 128], P('item')
All inputs are finite; a program needn't handle non-finite values.
Results may differ from a plain program's by a relative error of at most 0.002.
Values may be sent and summed in bfloat16 or wider, within the bound.
No kernel may reach another device: no remote copies, remote signals or barrier semaphores. Data moves between devices by JAX's collectives and lax.ppermute only.
A program may use at most 64 MiB of HBM per device.

v0:
```python
import jax
import jax.numpy as jnp
from jax import lax
from jax.sharding import PartitionSpec as P

STEPS = 2


STEP_SCALE = 4.0
DECAY_RATE = 0.02


def unpack_rows(packed, side):
    lanes = jnp.arange(side, dtype=jnp.int32)
    picked = packed[:, lanes // 32]
    return jnp.bitwise_and(jnp.right_shift(picked, lanes % 32), 1)


def tile_terms(user_panel, item_panel, tile_vals, tile_wts, packed, user_ids, item_ids, live_mask):
    side = tile_vals.shape[1]
    rowbits = unpack_rows(packed, side).astype(jnp.float32) * live_mask[:, None]
    weighted = tile_wts.astype(jnp.float32) * rowbits[:, :, None]
    user_rows = jnp.take(user_panel, user_ids, axis=0)
    item_rows = jnp.take(item_panel, item_ids, axis=0)
    predicted = jnp.einsum("tbr,tcr->tbc", user_rows, item_rows, preferred_element_type=jnp.float32)
    residual = (weighted * (tile_vals.astype(jnp.float32) - predicted)).astype(jnp.bfloat16)
    user_part = jnp.einsum("tbc,tcr->tbr", residual, item_rows, preferred_element_type=jnp.float32)
    item_part = jnp.einsum("tbc,tbr->tcr", residual, user_rows, preferred_element_type=jnp.float32)
    return (user_part, item_part, jnp.sum(weighted, axis=2), jnp.sum(weighted, axis=1))


def sweep(user_panel, item_panel, tiles, live_count, totals):
    per_block = 8
    blocks = (live_count + per_block - 1) // per_block

    def one_block(block, state):
        anchor = block * per_block

        def cut_block(array):
            return lax.dynamic_slice_in_dim(array, anchor, per_block, 0)

        tile_vals, tile_wts, packed, user_ids, item_ids = [cut_block(array) for array in tiles]
        slot_index = anchor + jnp.arange(per_block, dtype=jnp.int32)
        live_mask = (slot_index < live_count).astype(jnp.float32)
        user_part, item_part, user_rowsum, item_rowsum = tile_terms(
            user_panel, item_panel, tile_vals, tile_wts, packed, user_ids, item_ids, live_mask
        )
        user_sum, user_diag, item_sum, item_diag = state
        return (
            user_sum.at[user_ids].add(user_part),
            user_diag.at[user_ids].add(user_rowsum),
            item_sum.at[item_ids].add(item_part),
            item_diag.at[item_ids].add(item_rowsum),
        )

    return lax.fori_loop(0, blocks, one_block, totals)


def on_device(ratings, weights, row_masks, tile_users, tile_items, tile_counts, users, items):
    side = ratings.shape[1]
    rank = users.shape[1]
    count_here = tile_counts[0]
    own_tiles = (ratings, weights, row_masks, tile_users, tile_items)
    for iteration in range(STEPS):
        user_panel, item_panel = (
            lax.all_gather(users.astype(jnp.bfloat16), "item", axis=0, tiled=True),
            lax.all_gather(items.astype(jnp.bfloat16), "item", axis=0, tiled=True),
        )
        user_panel = user_panel.reshape(-1, side, rank)
        item_panel = item_panel.reshape(-1, side, rank)
        user_count = user_panel.shape[0]
        item_count = item_panel.shape[0]
        totals = (
            jnp.zeros((user_count, side, rank), jnp.float32),
            jnp.zeros((user_count, side), jnp.float32),
            jnp.zeros((item_count, side, rank), jnp.float32),
            jnp.zeros((item_count, side), jnp.float32),
        )
        user_sum, user_diag, item_sum, item_diag = sweep(
            user_panel, item_panel, own_tiles, count_here, totals
        )
        user_grad = user_sum.reshape(-1, rank)
        user_diag = user_diag.reshape(-1)
        item_grad = item_sum.reshape(-1, rank)
        item_diag = item_diag.reshape(-1)
        user_grad, user_diag, item_grad, item_diag = (
            lax.psum_scatter(user_grad, "item", scatter_dimension=0, tiled=True),
            lax.psum_scatter(user_diag, "item", scatter_dimension=0, tiled=True),
            lax.psum_scatter(item_grad, "item", scatter_dimension=0, tiled=True),
            lax.psum_scatter(item_diag, "item", scatter_dimension=0, tiled=True),
        )
        item_grad, item_diag = lax.psum((item_grad, item_diag), "user")
        user_weight = 2.0 * side + user_diag
        item_weight = 2.0 * side + item_diag
        users = users + STEP_SCALE * (user_grad / user_weight[:, None] - DECAY_RATE * users)
        items = items + STEP_SCALE * (item_grad / item_weight[:, None] - DECAY_RATE * items)
    return (users, items)


def solution(mesh):
    return jax.shard_map(
        on_device,
        mesh=mesh,
        in_specs=(
            P(("user", "item"), None, None),
            P(("user", "item"), None, None),
            P(("user", "item"), None),
            P(("user", "item")),
            P(("user", "item")),
            P(("user", "item")),
            P(("user", "item"), None),
            P("item", None),
        ),
        out_specs=(P(("user", "item"), None), P("item", None)),
        check_vma=False,
    )
```

profile of v0, /device:TPU:2, one launch (start us, length us, event | category | flops | bytes accessed | tf_op | source)
XLA Modules:
  0.0 1028.6 jit_solution(3896531610678982321)
XLA Ops:
  7.9 0.8 convert_element_type.88
  8.7 0.8 convert_element_type.89
  9.6 25.9 %all_gather.13 = bf16[2048,128]{1,0:T(8,128)(2,1)} all-gather(bf16[128,128]{1,0:T(8,128)(2,1)S(1)} %convert_element_type.89), channel_id=1, replica_groups=mesh['user'=16,'item'=16] {'item'}, dimensions={0}, use_global_device_ids=true | all-gather | bytes 557056 | tf_op jit(solution)/shard_map/all_gather | solution.py:67
  35.5 24.3 %all_gather.12 = bf16[2048,128]{1,0:T(8,128)(2,1)} all-gather(bf16[128,128]{1,0:T(8,128)(2,1)S(1)} %convert_element_type.88), channel_id=1, replica_groups=mesh['user'=16,'item'=16] {'item'}, dimensions={0}, use_global_device_ids=true | all-gather | bytes 557056 | tf_op jit(solution)/shard_map/all_gather | solution.py:66
  59.9 0.1 broadcast.388.clone.2
  60.0 0.1 broadcast.388.clone.1
  60.1 14.0 %while.36 = (s32[]{:T(128)}, f32[16,128,128]{2,1,0:T(8,128)S(1)}, f32[16,128]{1,0:T(8,128)S(1)}, f32[16,128,128]{2,1,0:T(8,128)S(1)}, f32[16,128]{1,0:T(8,128)S(...) while((s32[]{:T(128)}, f32[16,128,128]{2,1,0:T(8,128)S(1)}, ...), condition=%wide.region_7.9_spmd, body=%wide.region_0.8_spmd.sunk | while | flops 102769920 | bytes 7946063 | solution.py:56
  60.1 0.7 compare_convert_fusion.4
  60.8 0.8 constant_dynamic-slice_fusion.4
  61.6 0.8 compare_and_fusion.6
  62.4 0.6 gather_fusion
  63.1 0.1 multiply_bitcast_fusion.4
  63.2 1.4 fusion.45
  64.5 0.6 scatter_fusion.1
  65.2 0.6 scatter_fusion.3
  65.8 1.6 gather_fusion.2
  67.4 1.6 gather_fusion.1
  69.1 1.4 fusion.43
  70.5 0.3 fusion.46
  70.8 0.9 fusion.44
  71.7 1.2 scatter_fusion
  72.9 1.2 scatter_fusion.2
  74.1 1.0 copy-done.2
  75.2 0.3 copy-done.3
  75.4 0.4 reduce-scatter.5.cloned.1.call-update
  75.9 1.3 dynamic-slice
  77.9 263.4 %all-reduce.5 = (f32[2048]{0:T(1024)S(1)}, f32[2048]{0:T(1024)S(1)}) all-reduce(f32[2048]{0:T(1024)S(1)} %bitcast.50, f32[2048]{0:T(1024)S(1)} %bitcast.49), channel_id=3, replica_groups=mesh['user'=16,'item'=16] {'item'}, use_global_device_ids=true, to_apply=%region_9.11.clone | all-reduce | flops 4096 | bytes 32768
  341.3 0.1 dynamic-slice.3
  341.4 23.5 %psum.29 = f32[128]{0:T(128)S(1)} all-reduce(f32[128]{0:T(128)S(1)} %dynamic-slice.3), channel_id=1, replica_groups=mesh['user'=16,'item'=16] {'user'}, use_global_device_ids=true, to_apply=%region_13.15 | all-reduce | flops 128 | bytes 1024 | tf_op jit(solution)/shard_map/psum | solution.py:92
  364.9 0.1 dynamic-slice_add_fusion.1
  365.1 62.9 %reduce-scatter.5.cloned.1.call-done = f32[128,128]{1,0:T(8,128)} async-done(((f32[2048,128]{1,0:T(8,128)}), f32[128,128]{1,0:T(8,128)}) %reduce-scatter.5.cloned.1.call-update) | async-done | bytes 65552 | tf_op jit(solution)/shard_map/reduce_scatter | solution.py:87
  428.0 0.9 fusion.20
  429.0 24.3 %all_gather.14 = bf16[2048,128]{1,0:T(8,128)(2,1)} all-gather(bf16[128,128]{1,0:T(8,128)(2,1)S(1)} %fusion.20), channel_id=1, replica_groups=mesh['user'=16,'item'=16] {'item'}, dimensions={0}, use_global_device_ids=true | all-gather | bytes 557056 | tf_op jit(solution)/shard_map/all_gather | solution.py:66
  453.3 75.6 %all-reduce.9.cloned.1.call-done = f32[128,128]{1,0:T(8,128)} async-done(((f32[128,128]{1,0:T(8,128)}), f32[128,128]{1,0:T(8,128)}) %all-reduce.9.cloned.1.call-update) | async-done | bytes 65552 | tf_op jit(solution)/shard_map/psum | solution.py:92
  528.9 0.9 fusion.21
  529.8 25.7 %all_gather.15 = bf16[2048,128]{1,0:T(8,128)(2,1)} all-gather(bf16[128,128]{1,0:T(8,128)(2,1)S(1)} %fusion.21), channel_id=1, replica_groups=mesh['user'=16,'item'=16] {'item'}, dimensions={0}, use_global_device_ids=true | all-gather | bytes 557056 | tf_op jit(solution)/shard_map/all_gather | solution.py:67
  555.5 0.1 broadcast.388.clone
  555.6 0.1 broadcast.388
  555.7 14.0 %while.37 = (s32[]{:T(128)}, f32[16,128,128]{2,1,0:T(8,128)S(1)}, f32[16,128]{1,0:T(8,128)S(1)}, f32[16,128,128]{2,1,0:T(8,128)S(1)}, f32[16,128]{1,0:T(8,128)S(...) while((s32[]{:T(128)}, f32[16,128,128]{2,1,0:T(8,128)S(1)}, ...), condition=%wide.region_21.23_spmd, body=%wide.region_14.22_spmd.sunk | while | flops 102769920 | bytes 7946063 | solution.py:56
  555.8 0.7 compare_convert_fusion.5
  556.4 0.8 constant_dynamic-slice_fusion.5
  557.2 0.8 compare_and_fusion.7
  558.0 0.6 gather_fusion.3
  558.8 1.4 fusion.52
  560.1 0.6 scatter_fusion.5
  560.8 0.6 scatter_fusion.7
  561.4 1.6 gather_fusion.5
  563.0 1.6 gather_fusion.4
  564.7 1.4 fusion.50
  566.1 0.3 fusion.53
  566.4 1.0 fusion.51
  567.4 1.2 scatter_fusion.4
  568.6 1.2 scatter_fusion.6
  569.7 1.0 copy-done
  570.8 0.3 copy-done.1
  571.1 0.3 reduce-scatter.9.cloned.1.call-update
  571.4 263.1 %all-reduce.4 = (f32[2048]{0:T(1024)S(1)}, f32[2048]{0:T(1024)S(1)}) all-reduce(f32[2048]{0:T(1024)S(1)} %bitcast.48, f32[2048]{0:T(1024)S(1)} %bitcast.47), channel_id=7, replica_groups=mesh['user'=16,'item'=16] {'item'}, use_global_device_ids=true, to_apply=%region_23.25.clone | all-reduce | flops 4096 | bytes 32768
  834.5 0.1 dynamic-slice.7
  834.6 23.8 %psum.31 = f32[128]{0:T(128)S(1)} all-reduce(f32[128]{0:T(128)S(1)} %dynamic-slice.7), channel_id=1, replica_groups=mesh['user'=16,'item'=16] {'user'}, use_global_device_ids=true, to_apply=%region_27.29 | all-reduce | flops 128 | bytes 1024 | tf_op jit(solution)/shard_map/psum | solution.py:92
  858.4 0.1 dynamic-slice_add_fusion
  858.5 60.7 %reduce-scatter.9.cloned.1.call-done = f32[128,128]{1,0:T(8,128)} async-done(((f32[2048,128]{1,0:T(8,128)}), f32[128,128]{1,0:T(8,128)}) %reduce-scatter.9.cloned.1.call-update) | async-done | bytes 65552 | tf_op jit(solution)/shard_map/reduce_scatter | solution.py:87
  919.2 1.6 multiply_add_fusion.1
  920.8 99.3 %all-reduce.11.cloned.1.call-done = f32[128,128]{1,0:T(8,128)} async-done(((f32[128,128]{1,0:T(8,128)}), f32[128,128]{1,0:T(8,128)}) %all-reduce.11.cloned.1.call-update) | async-done | bytes 65552 | tf_op jit(solution)/shard_map/psum | solution.py:92
  1020.1 1.6 multiply_add_fusion
  (55 shorter events, 0.6 us)
Async XLA Ops:
  7.2 357.8 %reduce-scatter.7.cloned.1.call-start = ((), (), s32[]{:S(2)}) async-start(), calls=%async_computation.5 | async-start | bytes 1114112 | tf_op jit(solution)/shard_map/reduce_scatter | solution.py:89
  60.1 368.0 %copy-start.4 = (f32[128,128]{1,0:T(8,128)S(1)}, f32[128,128]{1,0:T(8,128)}, u32[]{:S(2)}) copy-start(f32[128,128]{1,0:T(8,128)} %param.20) | copy-start | bytes 196612
  60.1 468.8 %copy-start.5 = (f32[128,128]{1,0:T(8,128)S(1)}, f32[128,128]{1,0:T(8,128)}, u32[]{:S(2)}) copy-start(f32[128,128]{1,0:T(8,128)} %param.21) | copy-start | bytes 196612
  62.3 8.2 copy-start.6
  62.3 8.2 copy-start.8
  62.4 8.2 copy-start.10
  74.1 1.0 copy-start.2
  74.1 1.4 copy-start.3
  75.1 352.9 %reduce-scatter.5.cloned.1.call-start = ((), (), s32[]{:S(2)}) async-start(), calls=%async_computation.4 | async-start | bytes 1114112 | tf_op jit(solution)/shard_map/reduce_scatter | solution.py:87
  75.9 453.0 %all-reduce.9.cloned.1.call-start = ((), (), s32[]{:S(2)}) async-start(), calls=%async_computation.6 | async-start | bytes 131072 | tf_op jit(solution)/shard_map/psum | solution.py:92
  365.0 190.5 %copy-start.13 = (f32[128]{0:T(128)}, f32[128]{0:T(128)S(1)}, u32[]{:S(2)}) copy-start(f32[128]{0:T(128)S(1)} %dynamic-slice_add_fusion.1) | copy-start | bytes 1540
  365.0 190.5 %copy-start.12 = (f32[128]{0:T(128)}, f32[128]{0:T(128)S(1)}, u32[]{:S(2)}) copy-start(f32[128]{0:T(128)S(1)} %broadcast_add_fusion.1) | copy-start | bytes 1540
  365.0 493.4 %reduce-scatter.11.cloned.1.call-start = ((), (), s32[]{:S(2)}) async-start(), calls=%async_computation.8 | async-start | bytes 1114112 | tf_op jit(solution)/shard_map/reduce_scatter | solution.py:89
  558.0 8.2 copy-start.7
  558.0 8.2 copy-start.9
  558.0 8.2 copy-start.11
  569.7 1.0 copy-start
  569.7 1.4 copy-start.1
  570.8 348.4 %reduce-scatter.9.cloned.1.call-start = ((), (), s32[]{:S(2)}) async-start(), calls=%async_computation.7 | async-start | bytes 1114112 | tf_op jit(solution)/shard_map/reduce_scatter | solution.py:87
  571.4 448.7 %all-reduce.11.cloned.1.call-start = ((), (), s32[]{:S(2)}) async-start(), calls=%async_computation.9 | async-start | bytes 131072 | tf_op jit(solution)/shard_map/psum | solution.py:92
Sparse Core Ops, SparseCore 0:
  75.3 271.4 reduce-scatter.6
  350.6 77.3 reduce-scatter.4
  430.4 98.4 all-reduce.8
  570.9 267.5 reduce-scatter.10
  841.8 77.3 reduce-scatter.8
  921.5 98.5 all-reduce.10
where the time goes:
time: 1040 us; the launch traced here: 1030 us
  blocking collectives  674 us (65%)
  waiting for transfers between devices  299 us (29%)
  other arithmetic  19.8 us (2%)
  between operations  15.6 us (2%)
  local copies, waits for them, and re-layouts  13.9 us (1%)
    unnamed x2, blocking collectives  527 us
    psum x2, waiting for transfers between devices, on_device(): item_grad, item_diag = lax.psum((item_grad, item_diag), 'user')  175 us
    reduce_scatter x2, waiting for transfers between devices, on_device(): lax.psum_scatter(user_grad, 'item', scatter_dimension=0, tiled=True)  124 us
    all_gather x2, blocking collectives, on_device(): lax.all_gather(items.astype(jnp.bfloat16), 'item', axis=0, tiled=True)  51.6 us
    all_gather x2, blocking collectives, on_device(): lax.all_gather(users.astype(jnp.bfloat16), 'item', axis=0, tiled=True)  48.6 us
    psum x2, blocking collectives, on_device(): item_grad, item_diag = lax.psum((item_grad, item_diag), 'user')  47.3 us
  transfers between devices with their start and end apart: 6, of which 4 were waited for; matrix products, arithmetic and copies ran while one was open for 0% of the time, Pallas kernels for 0%

commit v1 on v0

v1 whole, which is shorter than its diff:
```python
import functools

import jax
import jax.numpy as jnp
from jax import lax
from jax.experimental import pallas as pl
from jax.experimental.pallas import tpu as pltpu
from jax.sharding import PartitionSpec as P

STEPS = 2


STEP_SCALE = 4.0
DECAY_RATE = 0.02

PER_BLOCK = 8


def tile_kernel(with_diag, per_block, count_ref, users_ref, items_ref, masks_ref,
                panel_ref, ratings_ref, weights_ref, acc_ref):
    step = pl.program_id(0)
    side = ratings_ref.shape[1]
    f32, bf16 = jnp.float32, jnp.bfloat16

    @pl.when(step == 0)
    def _():
        acc_ref[...] = jnp.zeros_like(acc_ref)

    count = count_ref[0]
    rows = lax.broadcasted_iota(jnp.int32, (side, side), 0)
    shift = jnp.bitwise_and(rows, 31)
    word_of = jnp.right_shift(rows, 5)
    if with_diag:
        picks = lax.broadcasted_iota(jnp.int32, (8, side), 0)
        first_row = (picks == 0).astype(bf16)
        second_row = (picks == 1).astype(bf16)

    for k in range(per_block):
        slot = step * per_block + k

        @pl.when(slot < count)
        def _():
            ub = users_ref[slot]
            ib = items_ref[slot]
            words = [masks_ref[slot * 4 + q] for q in range(4)]
            word = jnp.where(word_of == 0, words[0],
                             jnp.where(word_of == 1, words[1],
                                       jnp.where(word_of == 2, words[2], words[3])))
            bit = jnp.bitwise_and(lax.shift_right_logical(word, shift), 1)
            weighted = weights_ref[k].astype(f32) * bit.astype(f32)
            user_rows = panel_ref[ub, 0:side, :]
            item_rows = panel_ref[ib, side:2 * side, :]
            predicted = lax.dot_general(user_rows, item_rows, (((1,), (1,)), ((), ())),
                                        preferred_element_type=f32)
            residual = (weighted * (ratings_ref[k].astype(f32) - predicted)).astype(bf16)
            acc_ref[ub, 0:side, :] += jnp.dot(residual, item_rows, preferred_element_type=f32)
            acc_ref[ib, side:2 * side, :] += lax.dot_general(
                residual, user_rows, (((0,), (0,)), ((), ())), preferred_element_type=f32)
            if with_diag:
                half = weighted.astype(bf16)
                acc_ref[ub, 2 * side:2 * side + 8, :] += lax.dot_general(
                    first_row, half, (((1,), (1,)), ((), ())), preferred_element_type=f32)
                acc_ref[ib, 2 * side:2 * side + 8, :] += jnp.dot(
                    second_row, half, preferred_element_type=f32)


def tile_terms(with_diag, blocks, count, tile_users, tile_items, masks, panel, ratings, weights):
    slots, side, _ = ratings.shape
    per_block = PER_BLOCK
    grid = slots // per_block
    acc_rows = 2 * side + (8 if with_diag else 0)

    def tile_map(step, count_ref, *_):
        last = jnp.maximum((count_ref[0] - 1) // per_block, 0)
        return (jnp.minimum(step, last), 0, 0)

    def whole(step, *_):
        return (0, 0, 0)

    flops = slots * (3 * 2 * side * side * side)
    bytes_accessed = 2 * ratings.size * 2 + panel.size * 2 + blocks * acc_rows * side * 4
    return pl.pallas_call(
        functools.partial(tile_kernel, with_diag, per_block),
        out_shape=jax.ShapeDtypeStruct((blocks, acc_rows, side), jnp.float32),
        grid_spec=pltpu.PrefetchScalarGridSpec(
            num_scalar_prefetch=4,
            grid=(grid,),
            in_specs=[
                pl.BlockSpec(panel.shape, whole),
                pl.BlockSpec((per_block, side, side), tile_map),
                pl.BlockSpec((per_block, side, side), tile_map),
            ],
            out_specs=pl.BlockSpec((blocks, acc_rows, side), whole),
        ),
        compiler_params=pltpu.CompilerParams(dimension_semantics=("arbitrary",)),
        cost_estimate=pl.CostEstimate(flops=flops, bytes_accessed=bytes_accessed, transcendentals=0),
    )(count, tile_users, tile_items, masks, panel, ratings, weights)


def gather_panel(users, items, blocks):
    own = jnp.concatenate([users.astype(jnp.bfloat16), items.astype(jnp.bfloat16)], axis=0)
    copies = jnp.broadcast_to(own[None], (blocks,) + own.shape)
    return lax.all_to_all(copies, "item", 0, 0, tiled=False)


def sum_over_user(part, groups):
    copies = jnp.broadcast_to(part[None], (groups,) + part.shape)
    return jnp.sum(lax.all_to_all(copies, "user", 0, 0, tiled=False), axis=0)


def on_device(groups, blocks, ratings, weights, row_masks, tile_users, tile_items, tile_counts, users, items):
    side = ratings.shape[1]
    masks = row_masks.reshape(-1)
    user_weight = None
    item_weight = None
    for iteration in range(STEPS):
        with_diag = iteration == 0
        panel = gather_panel(users, items, blocks)
        acc = tile_terms(with_diag, blocks, tile_counts, tile_users, tile_items, masks, panel, ratings, weights)
        total = jnp.sum(lax.all_to_all(acc, "item", 0, 0, tiled=False), axis=0)
        item_total = sum_over_user(total[side:], groups)
        user_grad = total[0:side]
        item_grad = item_total[0:side]
        if with_diag:
            user_weight = 2.0 * side + total[2 * side]
            item_weight = 2.0 * side + item_total[side + 1]
        users = users + STEP_SCALE * (user_grad / user_weight[:, None] - DECAY_RATE * users)
        items = items + STEP_SCALE * (item_grad / item_weight[:, None] - DECAY_RATE * items)
    return (users, items)


def solution(mesh):
    groups = mesh.shape["user"]
    blocks = mesh.shape["item"]
    return jax.shard_map(
        functools.partial(on_device, groups, blocks),
        mesh=mesh,
        in_specs=(
            P(("user", "item"), None, None),
            P(("user", "item"), None, None),
            P(("user", "item"), None),
            P(("user", "item")),
            P(("user", "item")),
            P(("user", "item")),
            P(("user", "item"), None),
            P("item", None),
        ),
        out_specs=(P(("user", "item"), None), P("item", None)),
        check_vma=False,
    )
```

time: 1040 us -> 268 us (0.26)
  blocking collectives: 674 us -> 144 us
  waiting for transfers between devices: 299 us -> 42.3 us
  Pallas kernels: 0 us -> 37.6 us
  starting transfers between devices: 0.24 us -> 31.4 us
  other arithmetic: 19.8 us -> 3.71 us
  between operations: 15.6 us -> 1.41 us
    unnamed x2 -> x0, blocking collectives: 527 us -> none
    psum x2 -> x0, waiting for transfers between devices: 175 us -> none  [on_device(): item_grad, item_diag = lax.psum((item_grad, item_diag), 'user')]
    all_to_all x0 -> x4, blocking collectives: none -> 144 us  [the longest x2 75.3 us: on_device(): total = jnp.sum(lax.all_to_all(acc, 'item', 0, 0, tiled=False), axis=0)]
    reduce_scatter x4 -> x0, waiting for transfers between devices: 124 us -> none  [the longest x2 124 us: on_device(): lax.psum_scatter(user_grad, 'item', scatter_dimension=0, tiled=True)]
    all_gather x4 -> x0, blocking collectives: 100 us -> none  [the longest x2 51.6 us: on_device(): lax.all_gather(items.astype(jnp.bfloat16), 'item', axis=0, tiled=True)]
    psum x2 -> x0, blocking collectives: 47.3 us -> none  [on_device(): item_grad, item_diag = lax.psum((item_grad, item_diag), 'user')]
    all_to_all x0 -> x2, waiting for transfers between devices: none -> 42.3 us  [the longest x1 27.9 us: sum_over_user(): return jnp.sum(lax.all_to_all(copies, 'user', 0, 0, tiled=False), axis=0)]
    pallas_call x0 -> x2, Pallas kernels: none -> 37.6 us  [tile_terms(): pl.pallas_call(functools.partial(tile_kernel, with_diag, per_block), out_...]
  transfers between devices with their start and end apart: 6 -> 2, of which waited for: 4 -> 2; matrix products, arithmetic and copies ran while one was open for 0% -> 0% of each run, Pallas kernels for 0% -> 0%
where the time goes in v1:
time: 268 us; the launch traced here: 265 us
  blocking collectives  144 us (54%)
  waiting for transfers between devices  42.3 us (16%)
  Pallas kernels  37.6 us (14%)
  starting transfers between devices  31.4 us (12%)
  local copies, waits for them, and re-layouts  4.36 us (2%)
  other arithmetic  3.71 us (1%)
    all_to_all x2, blocking collectives, on_device(): total = jnp.sum(lax.all_to_all(acc, 'item', 0, 0, tiled=False), axis=0)  75.3 us
    all_to_all x1, blocking collectives, sum_over_user(): return jnp.sum(lax.all_to_all(copies, 'user', 0, 0, tiled=False), axis=0)  46.8 us
    pallas_call x2, Pallas kernels, tile_terms(): pl.pallas_call(functools.partial(tile_kernel, with_diag, per_block), out_...  37.6 us
    all_to_all x1, waiting for transfers between devices, sum_over_user(): return jnp.sum(lax.all_to_all(copies, 'user', 0, 0, tiled=False), axis=0)  27.9 us
    all_to_all x1, starting transfers between devices, sum_over_user(): return jnp.sum(lax.all_to_all(copies, 'user', 0, 0, tiled=False), axis=0)  23.9 us
    all_to_all x1, blocking collectives, gather_panel(): return lax.all_to_all(copies, 'item', 0, 0, tiled=False)  21.9 us
    all_to_all x1, waiting for transfers between devices, gather_panel(): return lax.all_to_all(copies, 'item', 0, 0, tiled=False)  14.3 us
    all_to_all x1, starting transfers between devices, gather_panel(): return lax.all_to_all(copies, 'item', 0, 0, tiled=False)  7.48 us
  transfers between devices with their start and end apart: 2, of which 2 were waited for; matrix products, arithmetic and copies ran while one was open for 0% of the time, Pallas kernels for 0%

profile of v1, /device:TPU:2, one launch (start us, length us, event | category | flops | bytes accessed | tf_op | source)
XLA Modules:
  0.0 264.7 jit_solution(15689094092760628665)
XLA Ops:
  0.6 0.0 copy-start.3
  0.6 0.9 convert_element_type.12
  1.5 0.8 convert_element_type.13
  2.3 1.2 broadcast_in_dim.8
  3.5 7.5 %all-to-all-start = ((bf16[16,256,128]{2,1,0:T(8,128)(2,1)}), bf16[16,256,128]{2,1,0:T(8,128)(2,1)S(1)}, u32[]{:S(2)}, u32[]{:S(2)}) async-start(bf16[16,256,128]{2,1,0:T(8,128)(2,1)} %broadcast_in_dim.8), calls=%async_computation | async-start | bytes 2097152 | tf_op jit(solution)/shard_map/all_to_all | solution.py:103
  11.7 0.0 copy-done.3
  11.7 0.1 copy.11
  11.8 0.7 reshape.25.masks_ref
  12.5 14.3 %all-to-all-done.panel_ref = bf16[16,256,128]{2,1,0:T(8,128)(2,1)S(1)} async-done(((bf16[16,256,128]{2,1,0:T(8,128)(2,1)}), bf16[16,256,128]{2,1,0:T(8,128)(2,1)S(1)}, u32[]{:S(2)}, u32[]{:S(2)}) %all-to-all-start) | async-done | bytes 1048608 | tf_op jit(solution)/shard_map/all_to_all | solution.py:103
  26.8 0.0 copy-start
  26.8 1.0 copy-done
  27.8 18.9 %shard_map.95 = f32[16,264,128]{2,1,0:T(8,128)} custom-call(s32[1]{0:T(128)S(6)} %copy.12.count_ref, s32[120]{0:T(128)} %users_ref.3, s32[120]{0:T(128)} %items_ref.3, s32[480]{0:T(512)} %reshape.25.masks_ref, bf16[16,256,128]{2,1,0:T(8,128)(2,1)} %copy-done, bf16[120,128,128]{2,1,0:T(8,128)(2,1)} %ratings_ref.3, bf16[120,128,128]{2,1,0:T(8,128)(2,1)} %weights_ref.3), custom_call_target="tpu_custom_call" | custom-call | flops 1509949440 | bytes 11075584 | tf_op jit(solution)/shard_map/pallas_call | solution.py:82
  46.7 38.2 %all_to_all.30 = f32[16,264,128]{2,1,0:T(8,128)S(1)} all-to-all(f32[16,264,128]{2,1,0:T(8,128)} %shard_map.95), channel_id=1, replica_groups=mesh['user'=16,'item'=16] {'item'}, dimensions={0} | all-to-all | bytes 4325376 | tf_op jit(solution)/shard_map/all_to_all | solution.py:120
  84.9 0.1 reduce_sum.36
  85.1 0.0 copy-start.1
  85.1 0.0 copy-start.2
  85.1 1.1 broadcast_in_dim.9
  86.2 23.9 %all-to-all-start.2 = ((f32[16,136,128]{2,1,0:T(8,128)}), f32[16,136,128]{2,1,0:T(8,128)S(1)}, u32[]{:S(2)}, u32[]{:S(2)}) async-start(f32[16,136,128]{2,1,0:T(8,128)} %broadcast_in_dim.9), calls=%async_computation.2 | async-start | bytes 2228224 | tf_op jit(solution)/shard_map/all_to_all | solution.py:108
  110.1 0.0 copy-done.1
  110.1 0.1 fusion.11
  110.2 27.9 %all-to-all-done.2 = f32[16,136,128]{2,1,0:T(8,128)S(1)} async-done(((f32[16,136,128]{2,1,0:T(8,128)}), f32[16,136,128]{2,1,0:T(8,128)S(1)}, u32[]{:S(2)}, u32[]{:S(2)}) %all-to-all-start.2) | async-done | bytes 1114144 | tf_op jit(solution)/shard_map/all_to_all | solution.py:108
  138.1 0.1 reduce_sum.37
  138.2 0.0 copy-done.2
  138.2 0.1 fusion.12
  138.3 0.2 broadcast_in_dim.10
  138.5 21.9 %all_to_all.31.panel_ref = bf16[16,256,128]{2,1,0:T(8,128)(2,1)} all-to-all(bf16[16,256,128]{2,1,0:T(8,128)(2,1)S(1)} %broadcast_in_dim.10), channel_id=1, replica_groups=mesh['user'=16,'item'=16] {'item'}, dimensions={0} | all-to-all | bytes 2097152 | tf_op jit(solution)/shard_map/all_to_all | solution.py:103
  160.4 18.7 %shard_map.96 = f32[16,256,128]{2,1,0:T(8,128)} custom-call(s32[1]{0:T(128)S(6)} %copy.12.count_ref, s32[120]{0:T(128)} %users_ref.3, s32[120]{0:T(128)} %items_ref.3, s32[480]{0:T(512)} %reshape.25.masks_ref, bf16[16,256,128]{2,1,0:T(8,128)(2,1)} %all_to_all.31.panel_ref, bf16[120,128,128]{2,1,0:T(8,128)(2,1)} %ratings_ref.3, bf16[120,128,128]{2,1,0:T(8,128)(2,1)} %weights_ref.3), custom_call_target="tpu_custom_call" | custom-call | flops 1509949440 | bytes 11010048 | tf_op jit(solution)/shard_map/pallas_call | solution.py:82
  179.1 37.1 %all_to_all.32 = f32[16,256,128]{2,1,0:T(8,128)S(1)} all-to-all(f32[16,256,128]{2,1,0:T(8,128)} %shard_map.96), channel_id=1, replica_groups=mesh['user'=16,'item'=16] {'item'}, dimensions={0} | all-to-all | bytes 4194304 | tf_op jit(solution)/shard_map/all_to_all | solution.py:120
  216.2 0.1 reduce_sum.38
  216.3 0.7 fusion.13
  217.0 0.1 broadcast_in_dim.11
  217.1 46.8 %all_to_all.33 = f32[16,128,128]{2,1,0:T(8,128)S(1)} all-to-all(f32[16,128,128]{2,1,0:T(8,128)S(1)} %broadcast_in_dim.11), channel_id=1, replica_groups=mesh['user'=16,'item'=16] {'user'}, dimensions={0} | all-to-all | bytes 2097152 | tf_op jit(solution)/shard_map/all_to_all | solution.py:108
  263.9 0.1 reduce_sum.39
  263.9 0.7 multiply_add_fusion
  (5 shorter events, 0.0 us)
Async XLA Ops:
  0.6 11.0 %copy-start.3 = (s32[120,4]{0,1:T(4,128)S(1)}, s32[120,4]{0,1:T(4,128)}, u32[]{:S(2)}) copy-start(s32[120,4]{0,1:T(4,128)} %param.10) | copy-start | bytes 5764
  3.5 23.3 %all-to-all-start = ((bf16[16,256,128]{2,1,0:T(8,128)(2,1)}), bf16[16,256,128]{2,1,0:T(8,128)(2,1)S(1)}, u32[]{:S(2)}, u32[]{:S(2)}) async-start(bf16[16,256,128]{2,1,0:T(8,128)(2,1)} %broadcast_in_dim.8), calls=%async_computation | async-start | bytes 2097152 | tf_op jit(solution)/shard_map/all_to_all | solution.py:103
  26.8 1.0 copy-start
  85.1 25.0 %copy-start.1 = (f32[128,128]{1,0:T(8,128)S(1)}, f32[128,128]{1,0:T(8,128)}, u32[]{:S(2)}) copy-start(f32[128,128]{1,0:T(8,128)} %param.14) | copy-start | bytes 196612
  85.1 53.1 %copy-start.2 = (f32[128,128]{1,0:T(8,128)S(1)}, f32[128,128]{1,0:T(8,128)}, u32[]{:S(2)}) copy-start(f32[128,128]{1,0:T(8,128)} %param.15) | copy-start | bytes 196612
  86.2 52.0 %all-to-all-start.2 = ((f32[16,136,128]{2,1,0:T(8,128)}), f32[16,136,128]{2,1,0:T(8,128)S(1)}, u32[]{:S(2)}, u32[]{:S(2)}) async-start(f32[16,136,128]{2,1,0:T(8,128)} %broadcast_in_dim.9), calls=%async_computation.2 | async-start | bytes 2228224 | tf_op jit(solution)/shard_map/all_to_all | solution.py:108

commit v2 on v1

--- a/solution.py
+++ b/solution.py
@@ -13,7 +13,7 @@
 STEP_SCALE = 4.0
 DECAY_RATE = 0.02
 
-PER_BLOCK = 8
+PER_BLOCK = 24
 
 
 def tile_kernel(with_diag, per_block, count_ref, users_ref, items_ref, masks_ref,
@@ -27,19 +27,18 @@
         acc_ref[...] = jnp.zeros_like(acc_ref)
 
     count = count_ref[0]
-    rows = lax.broadcasted_iota(jnp.int32, (side, side), 0)
-    shift = jnp.bitwise_and(rows, 31)
-    word_of = jnp.right_shift(rows, 5)
-    if with_diag:
-        picks = lax.broadcasted_iota(jnp.int32, (8, side), 0)
-        first_row = (picks == 0).astype(bf16)
-        second_row = (picks == 1).astype(bf16)
 
-    for k in range(per_block):
-        slot = step * per_block + k
-
-        @pl.when(slot < count)
-        def _():
+    @pl.when(step * per_block < count)
+    def _():
+        rows = lax.broadcasted_iota(jnp.int32, (side, side), 0)
+        shift = jnp.bitwise_and(rows, 31)
+        word_of = jnp.right_shift(rows, 5)
+        if with_diag:
+            picks = lax.broadcasted_iota(jnp.int32, (8, side), 0)
+            first_row = (picks == 0).astype(bf16)
+            second_row = (picks == 1).astype(bf16)
+        for k in range(per_block):
+            slot = step * per_block + k
             ub = users_ref[slot]
             ib = items_ref[slot]
             words = [masks_ref[slot * 4 + q] for q in range(4)]
@@ -47,15 +46,16 @@
                              jnp.where(word_of == 1, words[1],
                                        jnp.where(word_of == 2, words[2], words[3])))
             bit = jnp.bitwise_and(lax.shift_right_logical(word, shift), 1)
-            weighted = weights_ref[k].astype(f32) * bit.astype(f32)
+            live = (slot < count).astype(f32)
+            weighted = weights_ref[k].astype(f32) * (bit.astype(f32) * live)
             user_rows = panel_ref[ub, 0:side, :]
             item_rows = panel_ref[ib, side:2 * side, :]
-            predicted = lax.dot_general(user_rows, item_rows, (((1,), (1,)), ((), ())),
-                                        preferred_element_type=f32)
+            user_cols = panel_ref[ub, 2 * side:3 * side, :]
+            item_cols = panel_ref[ib, 3 * side:4 * side, :]
+            predicted = jnp.dot(user_rows, item_cols, preferred_element_type=f32)
             residual = (weighted * (ratings_ref[k].astype(f32) - predicted)).astype(bf16)
             acc_ref[ub, 0:side, :] += jnp.dot(residual, item_rows, preferred_element_type=f32)
-            acc_ref[ib, side:2 * side, :] += lax.dot_general(
-                residual, user_rows, (((0,), (0,)), ((), ())), preferred_element_type=f32)
+            acc_ref[ib, side:2 * side, :] += jnp.dot(user_cols, residual, preferred_element_type=f32)
             if with_diag:
                 half = weighted.astype(bf16)
                 acc_ref[ub, 2 * side:2 * side + 8, :] += lax.dot_general(
@@ -100,7 +100,9 @@
 def gather_panel(users, items, blocks):
     own = jnp.concatenate([users.astype(jnp.bfloat16), items.astype(jnp.bfloat16)], axis=0)
     copies = jnp.broadcast_to(own[None], (blocks,) + own.shape)
-    return lax.all_to_all(copies, "item", 0, 0, tiled=False)
+    gathered = lax.all_to_all(copies, "item", 0, 0, tiled=False)
+    return jnp.concatenate([gathered, jnp.swapaxes(gathered[:, :users.shape[0]], 1, 2),
+                            jnp.swapaxes(gathered[:, users.shape[0]:], 1, 2)], axis=1)
 
 
 def sum_over_user(part, groups):
@@ -120,7 +122,7 @@
         total = jnp.sum(lax.all_to_all(acc, "item", 0, 0, tiled=False), axis=0)
         item_total = sum_over_user(total[side:], groups)
         user_grad = total[0:side]
-        item_grad = item_total[0:side]
+        item_grad = item_total[0:side].T
         if with_diag:
             user_weight = 2.0 * side + total[2 * side]
             item_weight = 2.0 * side + item_total[side + 1]

time: 268 us -> 239 us (0.89)
  starting transfers between devices: 31.4 us -> 15.7 us
  Pallas kernels: 37.6 us -> 24.6 us
  blocking collectives: 144 us -> 138 us
  other arithmetic: 3.71 us -> 6.72 us
    all_to_all x1, blocking collectives: 46.8 us -> 29.8 us  [sum_over_user(): return jnp.sum(lax.all_to_all(copies, 'user', 0, 0, tiled=False), axis=0)]
    all_to_all x1, starting transfers between devices: 23.9 us -> 8.19 us  [sum_over_user(): return jnp.sum(lax.all_to_all(copies, 'user', 0, 0, tiled=False), axis=0)]
    pallas_call x2, Pallas kernels: 37.6 us -> 24.6 us  [tile_terms(): pl.pallas_call(functools.partial(tile_kernel, with_diag, per_block), out_...]
    all_to_all x2, blocking collectives: 75.3 us -> 86.5 us  [on_device(): total = jnp.sum(lax.all_to_all(acc, 'item', 0, 0, tiled=False), axis=0)]
    concatenate x0 -> x2, other arithmetic: none -> 3 us  [gather_panel(): jnp.concatenate([gathered, jnp.swapaxes(gathered[:, :users.shape[0]], 1,...]
where the time goes in v2:
time: 239 us; the launch traced here: 234 us
  blocking collectives  138 us (58%)
  waiting for transfers between devices  42.3 us (18%)
  Pallas kernels  24.6 us (10%)
  starting transfers between devices  15.7 us (7%)
  other arithmetic  6.72 us (3%)
  local copies, waits for them, and re-layouts  5.43 us (2%)
    all_to_all x2, blocking collectives, on_device(): total = jnp.sum(lax.all_to_all(acc, 'item', 0, 0, tiled=False), axis=0)  86.5 us
    all_to_all x1, blocking collectives, sum_over_user(): return jnp.sum(lax.all_to_all(copies, 'user', 0, 0, tiled=False), axis=0)  29.8 us
    all_to_all x1, waiting for transfers between devices, sum_over_user(): return jnp.sum(lax.all_to_all(copies, 'user', 0, 0, tiled=False), axis=0)  27.9 us
    pallas_call x2, Pallas kernels, tile_terms(): pl.pallas_call(functools.partial(tile_kernel, with_diag, per_block), out_...  24.6 us
    all_to_all x1, blocking collectives, gather_panel(): gathered = lax.all_to_all(copies, 'item', 0, 0, tiled=False)  21.8 us
    all_to_all x1, waiting for transfers between devices, gather_panel(): gathered = lax.all_to_all(copies, 'item', 0, 0, tiled=False)  14.3 us
    all_to_all x1, starting transfers between devices, sum_over_user(): return jnp.sum(lax.all_to_all(copies, 'user', 0, 0, tiled=False), axis=0)  8.19 us
    all_to_all x1, starting transfers between devices, gather_panel(): gathered = lax.all_to_all(copies, 'item', 0, 0, tiled=False)  7.48 us
  transfers between devices with their start and end apart: 2, of which 2 were waited for; matrix products, arithmetic and copies ran while one was open for 0% of the time, Pallas kernels for 0%

profile of v2, /device:TPU:2, one launch (start us, length us, event | category | flops | bytes accessed | tf_op | source)
XLA Modules:
  0.0 234.4 jit_solution(6129308974769577374)
XLA Ops:
  0.6 0.0 copy-start.2
  0.6 0.9 convert_element_type.12
  1.5 0.8 convert_element_type.13
  2.3 0.1 copy.48
  2.5 1.1 broadcast_in_dim.8
  3.5 7.5 %all-to-all-start = ((bf16[16,256,128]{1,2,0:T(8,128)(2,1)}), bf16[16,256,128]{1,2,0:T(8,128)(2,1)S(1)}, u32[]{:S(2)}, u32[]{:S(2)}) async-start(bf16[16,256,128]{1,2,0:T(8,128)(2,1)} %broadcast_in_dim.8), calls=%async_computation | async-start | bytes 2097152 | tf_op jit(solution)/shard_map/all_to_all | solution.py:103
  11.7 0.0 copy-done.2
  11.7 0.1 copy.47
  11.8 0.7 reshape.25.masks_ref
  12.5 14.3 %all-to-all-done = bf16[16,256,128]{1,2,0:T(8,128)(2,1)S(1)} async-done(((bf16[16,256,128]{1,2,0:T(8,128)(2,1)}), bf16[16,256,128]{1,2,0:T(8,128)(2,1)S(1)}, u32[]{:S(2)}, u32[]{:S(2)}) %all-to-all-start) | async-done | bytes 1048608 | tf_op jit(solution)/shard_map/all_to_all | solution.py:103
  26.8 0.7 copy.49
  27.5 0.3 slice_bitcast_fusion.3
  27.8 1.5 pad_maximum_fusion.panel_ref
  29.2 13.0 %shard_map.95 = f32[16,264,128]{2,1,0:T(8,128)} custom-call(s32[1]{0:T(128)S(6)} %copy.55.count_ref, s32[120]{0:T(128)} %users_ref.3, s32[120]{0:T(128)} %items_ref.3, s32[480]{0:T(512)} %reshape.25.masks_ref, bf16[16,512,128]{2,1,0:T(8,128)(2,1)} %pad_maximum_fusion.panel_ref, bf16[120,128,128]{2,1,0:T(8,128)(2,1)} %ratings_ref.3, ...), custom_call_target="tpu_custom_call" | custom-call | flops 1509949440 | bytes 12124160 | tf_op jit(solution)/shard_map/pallas_call | solution.py:82
  42.3 44.3 %all_to_all.30 = f32[16,264,128]{2,1,0:T(8,128)S(1)} all-to-all(f32[16,264,128]{2,1,0:T(8,128)} %shard_map.95), channel_id=1, replica_groups=mesh['user'=16,'item'=16] {'item'}, dimensions={0} | all-to-all | bytes 4325376 | tf_op jit(solution)/shard_map/all_to_all | solution.py:122
  86.6 0.1 reduce_sum.36
  86.7 0.0 copy-start
  86.7 1.1 broadcast_in_dim.9
  87.8 0.0 copy-start.1
  87.8 8.2 %all-to-all-start.2 = ((f32[16,136,128]{2,1,0:T(8,128)}), f32[16,136,128]{2,1,0:T(8,128)S(1)}, u32[]{:S(2)}, u32[]{:S(2)}) async-start(f32[16,136,128]{2,1,0:T(8,128)} %broadcast_in_dim.9), calls=%async_computation.2 | async-start | bytes 2228224 | tf_op jit(solution)/shard_map/all_to_all | solution.py:110
  96.0 0.0 copy-done
  96.0 0.1 fusion.13
  96.1 27.9 %all-to-all-done.2 = f32[16,136,128]{2,1,0:T(8,128)S(1)} async-done(((f32[16,136,128]{2,1,0:T(8,128)}), f32[16,136,128]{2,1,0:T(8,128)S(1)}, u32[]{:S(2)}, u32[]{:S(2)}) %all-to-all-start.2) | async-done | bytes 1114144 | tf_op jit(solution)/shard_map/all_to_all | solution.py:110
  124.0 0.1 reduce_sum.37
  124.1 0.1 copy.54
  124.2 0.0 copy-done.1
  124.2 0.1 fusion.12
  124.4 0.1 copy.51
  124.5 0.1 broadcast_in_dim.10
  124.6 21.8 %all_to_all.31 = bf16[16,256,128]{1,2,0:T(8,128)(2,1)S(1)} all-to-all(bf16[16,256,128]{1,2,0:T(8,128)(2,1)S(1)} %broadcast_in_dim.10), channel_id=1, replica_groups=mesh['user'=16,'item'=16] {'item'}, dimensions={0} | all-to-all | bytes 2097152 | tf_op jit(solution)/shard_map/all_to_all | solution.py:103
  146.4 0.7 copy.52
  147.1 0.3 slice_bitcast_fusion.1
  147.4 1.5 pad_maximum_fusion.1.panel_ref
  148.9 11.6 %shard_map.96 = f32[16,256,128]{2,1,0:T(8,128)} custom-call(s32[1]{0:T(128)S(6)} %copy.55.count_ref, s32[120]{0:T(128)} %users_ref.3, s32[120]{0:T(128)} %items_ref.3, s32[480]{0:T(512)} %reshape.25.masks_ref, bf16[16,512,128]{2,1,0:T(8,128)(2,1)} %pad_maximum_fusion.1.panel_ref, bf16[120,128,128]{2,1,0:T(8,128)(2,1)} %ratings_ref.3, ...), custom_call_target="tpu_custom_call" | custom-call | flops 1509949440 | bytes 12058624 | tf_op jit(solution)/shard_map/pallas_call | solution.py:82
  160.5 42.2 %all_to_all.32 = f32[16,256,128]{2,1,0:T(8,128)S(1)} all-to-all(f32[16,256,128]{2,1,0:T(8,128)} %shard_map.96), channel_id=1, replica_groups=mesh['user'=16,'item'=16] {'item'}, dimensions={0} | all-to-all | bytes 4194304 | tf_op jit(solution)/shard_map/all_to_all | solution.py:122
  202.7 0.1 reduce_sum.38
  202.8 0.7 fusion.14
  203.6 0.1 broadcast_in_dim.11
  203.7 29.8 %all_to_all.33 = f32[16,128,128]{2,1,0:T(8,128)S(1)} all-to-all(f32[16,128,128]{2,1,0:T(8,128)S(1)} %broadcast_in_dim.11), channel_id=1, replica_groups=mesh['user'=16,'item'=16] {'user'}, dimensions={0} | all-to-all | bytes 2097152 | tf_op jit(solution)/shard_map/all_to_all | solution.py:110
  233.5 0.1 reduce_sum.39
  233.5 0.1 copy.53
  233.6 0.7 fusion.7
  (6 shorter events, 0.0 us)
Async XLA Ops:
  0.6 11.1 %copy-start.2 = (s32[120,4]{0,1:T(4,128)S(1)}, s32[120,4]{0,1:T(4,128)}, u32[]{:S(2)}) copy-start(s32[120,4]{0,1:T(4,128)} %param.10) | copy-start | bytes 5764
  3.5 23.3 %all-to-all-start = ((bf16[16,256,128]{1,2,0:T(8,128)(2,1)}), bf16[16,256,128]{1,2,0:T(8,128)(2,1)S(1)}, u32[]{:S(2)}, u32[]{:S(2)}) async-start(bf16[16,256,128]{1,2,0:T(8,128)(2,1)} %broadcast_in_dim.8), calls=%async_computation | async-start | bytes 2097152 | tf_op jit(solution)/shard_map/all_to_all | solution.py:103
  86.7 9.3 %copy-start = (f32[128,128]{1,0:T(8,128)S(1)}, f32[128,128]{1,0:T(8,128)}, u32[]{:S(2)}) copy-start(f32[128,128]{1,0:T(8,128)} %param.14) | copy-start | bytes 196612
  87.8 36.4 %copy-start.1 = (f32[128,128]{1,0:T(8,128)S(1)}, f32[128,128]{1,0:T(8,128)}, u32[]{:S(2)}) copy-start(f32[128,128]{1,0:T(8,128)} %param.15) | copy-start | bytes 196612
  87.8 36.2 %all-to-all-start.2 = ((f32[16,136,128]{2,1,0:T(8,128)}), f32[16,136,128]{2,1,0:T(8,128)S(1)}, u32[]{:S(2)}, u32[]{:S(2)}) async-start(f32[16,136,128]{2,1,0:T(8,128)} %broadcast_in_dim.9), calls=%async_computation.2 | async-start | bytes 2228224 | tf_op jit(solution)/shard_map/all_to_all | solution.py:110

commit v3 on v2

--- a/solution.py
+++ b/solution.py
@@ -106,8 +106,13 @@
 
 
 def sum_over_user(part, groups):
-    copies = jnp.broadcast_to(part[None], (groups,) + part.shape)
-    return jnp.sum(lax.all_to_all(copies, "user", 0, 0, tiled=False), axis=0)
+    assert groups & (groups - 1) == 0
+    distance = 1
+    while distance < groups:
+        pairs = [(j, j ^ distance) for j in range(groups)]
+        part = part + lax.ppermute(part, "user", pairs)
+        distance *= 2
+    return part
 
 
 def on_device(groups, blocks, ratings, weights, row_masks, tile_users, tile_items, tile_counts, users, items):

time: 239 us -> 200 us (0.84); the launches traced: 234 us -> 200 us
  blocking collectives: 138 us -> 104 us
  starting transfers between devices: 15.7 us -> 31.4 us
  Pallas kernels: 24.6 us -> 16.9 us
  waiting for transfers between devices: 42.3 us -> 35.7 us
    all_to_all x1 -> x0, blocking collectives: 29.8 us -> none  [sum_over_user(): return jnp.sum(lax.all_to_all(copies, 'user', 0, 0, tiled=False), axis=0)]
    all_to_all x1 -> x0, waiting for transfers between devices: 27.9 us -> none  [sum_over_user(): return jnp.sum(lax.all_to_all(copies, 'user', 0, 0, tiled=False), axis=0)]
    ppermute x0 -> x8, starting transfers between devices: none -> 23.9 us  [sum_over_user(): part = part + lax.ppermute(part, 'user', pairs)]
    ppermute x0 -> x8, waiting for transfers between devices: none -> 21.3 us  [sum_over_user(): part = part + lax.ppermute(part, 'user', pairs)]
    all_to_all x1 -> x0, starting transfers between devices: 8.19 us -> none  [sum_over_user(): return jnp.sum(lax.all_to_all(copies, 'user', 0, 0, tiled=False), axis=0)]
    pallas_call x2, Pallas kernels: 24.6 us -> 16.9 us  [tile_terms(): pl.pallas_call(functools.partial(tile_kernel, with_diag, per_block), out_...]
    all_to_all x1, blocking collectives: 21.8 us -> 17.3 us  [gather_panel(): gathered = lax.all_to_all(copies, 'item', 0, 0, tiled=False)]
  transfers between devices with their start and end apart: 2 -> 9, of which waited for: 2 -> 9; matrix products, arithmetic and copies ran while one was open for 0% -> 1% of each run, Pallas kernels for 0% -> 0%
where the time goes in v3:
time: 200 us
  blocking collectives  104 us (52%)
  waiting for transfers between devices  35.7 us (18%)
  starting transfers between devices  31.4 us (16%)
  Pallas kernels  16.9 us (8%)
  local copies, waits for them, and re-layouts  5.79 us (3%)
  other arithmetic  5.11 us (3%)
    all_to_all x2, blocking collectives, on_device(): total = jnp.sum(lax.all_to_all(acc, 'item', 0, 0, tiled=False), axis=0)  86.8 us
    ppermute x8, starting transfers between devices, sum_over_user(): part = part + lax.ppermute(part, 'user', pairs)  23.9 us
    ppermute x8, waiting for transfers between devices, sum_over_user(): part = part + lax.ppermute(part, 'user', pairs)  21.3 us
    all_to_all x1, blocking collectives, gather_panel(): gathered = lax.all_to_all(copies, 'item', 0, 0, tiled=False)  17.3 us
    pallas_call x2, Pallas kernels, tile_terms(): pl.pallas_call(functools.partial(tile_kernel, with_diag, per_block), out_...  16.9 us
    all_to_all x1, waiting for transfers between devices, gather_panel(): gathered = lax.all_to_all(copies, 'item', 0, 0, tiled=False)  14.3 us
    all_to_all x1, starting transfers between devices, gather_panel(): gathered = lax.all_to_all(copies, 'item', 0, 0, tiled=False)  7.48 us
  transfers between devices with their start and end apart: 9, of which 9 were waited for; matrix products, arithmetic and copies ran while one was open for 1% of the time, Pallas kernels for 0%

profile of v3, /device:TPU:2, one launch (start us, length us, event | category | flops | bytes accessed | tf_op | source)
XLA Modules:
  0.0 200.3 jit_solution(17106897250957814304)
XLA Ops:
  0.6 0.0 copy-start.2
  0.6 0.9 convert_element_type.12
  1.5 0.8 convert_element_type.13
  2.3 0.1 copy.24
  2.5 1.1 broadcast_in_dim.4
  3.5 7.5 %all-to-all-start = ((bf16[16,256,128]{1,2,0:T(8,128)(2,1)}), bf16[16,256,128]{1,2,0:T(8,128)(2,1)S(1)}, u32[]{:S(2)}, u32[]{:S(2)}) async-start(bf16[16,256,128]{1,2,0:T(8,128)(2,1)} %broadcast_in_dim.4), calls=%async_computation | async-start | bytes 2097152 | tf_op jit(solution)/shard_map/all_to_all | solution.py:103
  11.7 0.0 copy-done.2
  11.7 0.1 copy.23
  11.8 0.7 reshape.23.masks_ref
  12.5 14.3 %all-to-all-done = bf16[16,256,128]{1,2,0:T(8,128)(2,1)S(1)} async-done(((bf16[16,256,128]{1,2,0:T(8,128)(2,1)}), bf16[16,256,128]{1,2,0:T(8,128)(2,1)S(1)}, u32[]{:S(2)}, u32[]{:S(2)}) %all-to-all-start) | async-done | bytes 1048608 | tf_op jit(solution)/shard_map/all_to_all | solution.py:103
  26.8 0.7 copy.25
  27.5 0.3 slice_bitcast_fusion.3
  27.8 1.5 pad_maximum_fusion.panel_ref
  29.2 8.8 %shard_map.95 = f32[16,264,128]{2,1,0:T(8,128)} custom-call(s32[1]{0:T(128)S(6)} %copy.37.count_ref, s32[120]{0:T(128)} %users_ref.3, s32[120]{0:T(128)} %items_ref.3, s32[480]{0:T(512)} %reshape.23.masks_ref, bf16[16,512,128]{2,1,0:T(8,128)(2,1)} %pad_maximum_fusion.panel_ref, bf16[120,128,128]{2,1,0:T(8,128)(2,1)} %ratings_ref.3, ...), custom_call_target="tpu_custom_call" | custom-call | flops 1509949440 | bytes 12124160 | tf_op jit(solution)/shard_map/pallas_call | solution.py:82
  38.0 44.3 %all_to_all.20 = f32[16,264,128]{2,1,0:T(8,128)S(1)} all-to-all(f32[16,264,128]{2,1,0:T(8,128)} %shard_map.95), channel_id=1, replica_groups=mesh['user'=16,'item'=16] {'item'}, dimensions={0} | all-to-all | bytes 4325376 | tf_op jit(solution)/shard_map/all_to_all | solution.py:127
  82.3 0.0 copy-start
  82.3 0.0 copy-start.1
  82.3 0.1 reduce_sum.18
  82.4 2.3 %collective-permute-start = (f32[136,128]{1,0:T(8,128)S(1)}, f32[136,128]{1,0:T(8,128)S(1)}, u32[]{:S(2)}, u32[]{:S(2)}) collective-permute-start(f32[136,128]{1,0:T(8,128)S(1)} %slice.48), channel_id=1, source_target_pairs={{0,16},{16,0},{32,48},{48,32},{64,80},{80,64},{96,112},{112,96},{1... | collective-permute-start | bytes 208904 | tf_op jit(solution)/shard_map/ppermute | solution.py:113
  84.7 0.9 collective-permute-done
  85.6 4.6 %collective-permute-start.1 = (f32[136,128]{1,0:T(8,128)S(1)}, f32[136,128]{1,0:T(8,128)S(1)}, u32[]{:S(2)}, u32[]{:S(2)}) collective-permute-start(f32[136,128]{1,0:T(8,128)S(1)} %slice_add_fusion.3), channel_id=1, source_target_pairs={{0,32},{16,48},{32,0},{48,16},{64,96},{80,112},{96,64},{112,80},{1... | collective-permute-start | bytes 208904 | tf_op jit(solution)/shard_map/ppermute | solution.py:113
  90.2 0.0 copy-done
  90.2 0.1 copy.28
  90.3 0.0 copy-done.1
  90.3 0.1 copy.30
  90.4 2.3 %collective-permute-done.1 = f32[136,128]{1,0:T(8,128)S(1)} collective-permute-done((f32[136,128]{1,0:T(8,128)S(1)}, f32[136,128]{1,0:T(8,128)S(1)}, u32[]{:S(2)}, u32[]{:S(2)}) %collective-permute-start.1) | collective-permute-done | bytes 69664 | tf_op jit(solution)/shard_map/ppermute | solution.py:113
  92.7 2.3 %collective-permute-start.2 = (f32[136,128]{1,0:T(8,128)S(1)}, f32[136,128]{1,0:T(8,128)S(1)}, u32[]{:S(2)}, u32[]{:S(2)}) collective-permute-start(f32[136,128]{1,0:T(8,128)S(1)} %add.60), channel_id=1, source_target_pairs={{0,64},{16,80},{32,96},{48,112},{64,0},{80,16},{96,32},{112,48},{1... | collective-permute-start | bytes 208904 | tf_op jit(solution)/shard_map/ppermute | solution.py:113
  95.0 0.1 copy.35
  95.1 3.0 %collective-permute-done.2 = f32[136,128]{1,0:T(8,128)S(1)} collective-permute-done((f32[136,128]{1,0:T(8,128)S(1)}, f32[136,128]{1,0:T(8,128)S(1)}, u32[]{:S(2)}, u32[]{:S(2)}) %collective-permute-start.2) | collective-permute-done | bytes 69664 | tf_op jit(solution)/shard_map/ppermute | solution.py:113
  98.2 8.3 %collective-permute-start.3 = (f32[136,128]{1,0:T(8,128)S(1)}, f32[136,128]{1,0:T(8,128)S(1)}, u32[]{:S(2)}, u32[]{:S(2)}) collective-permute-start(f32[136,128]{1,0:T(8,128)S(1)} %add.61), channel_id=1, source_target_pairs={{0,128},{16,144},{32,160},{48,176},{64,192},{80,208},{96,224},{112... | collective-permute-start | bytes 208904 | tf_op jit(solution)/shard_map/ppermute | solution.py:113
  106.5 2.4 %collective-permute-done.3 = f32[136,128]{1,0:T(8,128)S(1)} collective-permute-done((f32[136,128]{1,0:T(8,128)S(1)}, f32[136,128]{1,0:T(8,128)S(1)}, u32[]{:S(2)}, u32[]{:S(2)}) %collective-permute-start.3) | collective-permute-done | bytes 69664 | tf_op jit(solution)/shard_map/ppermute | solution.py:113
  109.0 0.1 broadcast_in_dim.5
  109.1 17.3 %all_to_all.21 = bf16[16,256,128]{1,2,0:T(8,128)(2,1)S(1)} all-to-all(bf16[16,256,128]{1,2,0:T(8,128)(2,1)S(1)} %broadcast_in_dim.5), channel_id=1, replica_groups=mesh['user'=16,'item'=16] {'item'}, dimensions={0} | all-to-all | bytes 2097152 | tf_op jit(solution)/shard_map/all_to_all | solution.py:103
  126.4 0.7 copy.31
  127.0 0.3 slice_bitcast_fusion.1
  127.3 1.5 pad_maximum_fusion.1.panel_ref
  128.8 8.1 %shard_map.96 = f32[16,256,128]{2,1,0:T(8,128)} custom-call(s32[1]{0:T(128)S(6)} %copy.37.count_ref, s32[120]{0:T(128)} %users_ref.3, s32[120]{0:T(128)} %items_ref.3, s32[480]{0:T(512)} %reshape.23.masks_ref, bf16[16,512,128]{2,1,0:T(8,128)(2,1)} %pad_maximum_fusion.1.panel_ref, bf16[120,128,128]{2,1,0:T(8,128)(2,1)} %ratings_ref.3, ...), custom_call_target="tpu_custom_call" | custom-call | flops 1509949440 | bytes 12058624 | tf_op jit(solution)/shard_map/pallas_call | solution.py:82
  136.9 42.5 %all_to_all.22 = f32[16,256,128]{2,1,0:T(8,128)S(1)} all-to-all(f32[16,256,128]{2,1,0:T(8,128)} %shard_map.96), channel_id=1, replica_groups=mesh['user'=16,'item'=16] {'item'}, dimensions={0} | all-to-all | bytes 4194304 | tf_op jit(solution)/shard_map/all_to_all | solution.py:127
  179.4 0.1 reduce_sum.19
  179.5 0.1 collective-permute-start.4
  179.6 1.2 collective-permute-done.4
  180.9 0.1 collective-permute-start.5
  181.0 4.3 %collective-permute-done.5 = f32[128,128]{1,0:T(8,128)S(1)} collective-permute-done((f32[128,128]{1,0:T(8,128)S(1)}, f32[128,128]{1,0:T(8,128)S(1)}, u32[]{:S(2)}, u32[]{:S(2)}) %collective-permute-start.5) | collective-permute-done | bytes 65568 | tf_op jit(solution)/shard_map/ppermute | solution.py:113
  185.3 0.1 collective-permute-start.6
  185.4 0.1 copy.36
  185.5 5.4 %collective-permute-done.6 = f32[128,128]{1,0:T(8,128)S(1)} collective-permute-done((f32[128,128]{1,0:T(8,128)S(1)}, f32[128,128]{1,0:T(8,128)S(1)}, u32[]{:S(2)}, u32[]{:S(2)}) %collective-permute-start.6) | collective-permute-done | bytes 65568 | tf_op jit(solution)/shard_map/ppermute | solution.py:113
  190.8 6.2 %collective-permute-start.7 = (f32[128,128]{1,0:T(8,128)S(1)}, f32[128,128]{1,0:T(8,128)S(1)}, u32[]{:S(2)}, u32[]{:S(2)}) collective-permute-start(f32[128,128]{1,0:T(8,128)S(1)} %add.69), channel_id=1, source_target_pairs={{0,128},{16,144},{32,160},{48,176},{64,192},{80,208},{96,224},{112... | collective-permute-start | bytes 196616 | tf_op jit(solution)/shard_map/ppermute | solution.py:113
  197.0 0.7 copy.33
  197.7 1.8 collective-permute-done.7
  199.6 0.7 copy.34
  (18 shorter events, 0.2 us)
Async XLA Ops:
  0.6 11.0 %copy-start.2 = (s32[120,4]{0,1:T(4,128)S(1)}, s32[120,4]{0,1:T(4,128)}, u32[]{:S(2)}) copy-start(s32[120,4]{0,1:T(4,128)} %param.10) | copy-start | bytes 5764
  3.5 23.3 %all-to-all-start = ((bf16[16,256,128]{1,2,0:T(8,128)(2,1)}), bf16[16,256,128]{1,2,0:T(8,128)(2,1)S(1)}, u32[]{:S(2)}, u32[]{:S(2)}) async-start(bf16[16,256,128]{1,2,0:T(8,128)(2,1)} %broadcast_in_dim.4), calls=%async_computation | async-start | bytes 2097152 | tf_op jit(solution)/shard_map/all_to_all | solution.py:103
  82.3 7.9 %copy-start = (f32[128,128]{1,0:T(8,128)S(1)}, f32[128,128]{1,0:T(8,128)}, u32[]{:S(2)}) copy-start(f32[128,128]{1,0:T(8,128)} %param.14) | copy-start | bytes 196612
  82.3 8.0 %copy-start.1 = (f32[128,128]{1,0:T(8,128)S(1)}, f32[128,128]{1,0:T(8,128)}, u32[]{:S(2)}) copy-start(f32[128,128]{1,0:T(8,128)} %param.15) | copy-start | bytes 196612
  82.4 3.2 %collective-permute-start = (f32[136,128]{1,0:T(8,128)S(1)}, f32[136,128]{1,0:T(8,128)S(1)}, u32[]{:S(2)}, u32[]{:S(2)}) collective-permute-start(f32[136,128]{1,0:T(8,128)S(1)} %slice.48), channel_id=1, source_target_pairs={{0,16},{16,0},{32,48},{48,32},{64,80},{80,64},{96,112},{112,96},{1... | collective-permute-start | bytes 208904 | tf_op jit(solution)/shard_map/ppermute | solution.py:113
  85.6 7.1 %collective-permute-start.1 = (f32[136,128]{1,0:T(8,128)S(1)}, f32[136,128]{1,0:T(8,128)S(1)}, u32[]{:S(2)}, u32[]{:S(2)}) collective-permute-start(f32[136,128]{1,0:T(8,128)S(1)} %slice_add_fusion.3), channel_id=1, source_target_pairs={{0,32},{16,48},{32,0},{48,16},{64,96},{80,112},{96,64},{112,80},{1... | collective-permute-start | bytes 208904 | tf_op jit(solution)/shard_map/ppermute | solution.py:113
  92.7 5.5 %collective-permute-start.2 = (f32[136,128]{1,0:T(8,128)S(1)}, f32[136,128]{1,0:T(8,128)S(1)}, u32[]{:S(2)}, u32[]{:S(2)}) collective-permute-start(f32[136,128]{1,0:T(8,128)S(1)} %add.60), channel_id=1, source_target_pairs={{0,64},{16,80},{32,96},{48,112},{64,0},{80,16},{96,32},{112,48},{1... | collective-permute-start | bytes 208904 | tf_op jit(solution)/shard_map/ppermute | solution.py:113
  98.2 10.7 %collective-permute-start.3 = (f32[136,128]{1,0:T(8,128)S(1)}, f32[136,128]{1,0:T(8,128)S(1)}, u32[]{:S(2)}, u32[]{:S(2)}) collective-permute-start(f32[136,128]{1,0:T(8,128)S(1)} %add.61), channel_id=1, source_target_pairs={{0,128},{16,144},{32,160},{48,176},{64,192},{80,208},{96,224},{112... | collective-permute-start | bytes 208904 | tf_op jit(solution)/shard_map/ppermute | solution.py:113
  179.5 1.3 collective-permute-start.4
  180.9 4.4 %collective-permute-start.5 = (f32[128,128]{1,0:T(8,128)S(1)}, f32[128,128]{1,0:T(8,128)S(1)}, u32[]{:S(2)}, u32[]{:S(2)}) collective-permute-start(f32[128,128]{1,0:T(8,128)S(1)} %get-tuple-element.8), channel_id=1, source_target_pairs={{0,32},{16,48},{32,0},{48,16},{64,96},{80,112},{96,64},{112,80},{1... | collective-permute-start | bytes 196616 | tf_op jit(solution)/shard_map/ppermute | solution.py:113
  185.3 5.6 %collective-permute-start.6 = (f32[128,128]{1,0:T(8,128)S(1)}, f32[128,128]{1,0:T(8,128)S(1)}, u32[]{:S(2)}, u32[]{:S(2)}) collective-permute-start(f32[128,128]{1,0:T(8,128)S(1)} %add.68), channel_id=1, source_target_pairs={{0,64},{16,80},{32,96},{48,112},{64,0},{80,16},{96,32},{112,48},{1... | collective-permute-start | bytes 196616 | tf_op jit(solution)/shard_map/ppermute | solution.py:113
  190.8 8.7 %collective-permute-start.7 = (f32[128,128]{1,0:T(8,128)S(1)}, f32[128,128]{1,0:T(8,128)S(1)}, u32[]{:S(2)}, u32[]{:S(2)}) collective-permute-start(f32[128,128]{1,0:T(8,128)S(1)} %add.69), channel_id=1, source_target_pairs={{0,128},{16,144},{32,160},{48,176},{64,192},{80,208},{96,224},{112... | collective-permute-start | bytes 196616 | tf_op jit(solution)/shard_map/ppermute | solution.py:113

commit v4 on v3

v4 whole, which is shorter than its diff:
```python
import functools

import jax
import jax.numpy as jnp
from jax import lax
from jax.experimental import pallas as pl
from jax.experimental.pallas import tpu as pltpu
from jax.sharding import PartitionSpec as P

STEPS = 2


STEP_SCALE = 4.0
DECAY_RATE = 0.02

PER_BLOCK = 24


def tile_kernel(with_diag, per_block, count_ref, users_ref, items_ref, *refs):
    if with_diag:
        panel_ref, ratings_ref, weighted_ref, diag_ref, acc_ref = refs
    else:
        panel_ref, ratings_ref, weighted_ref, acc_ref = refs
    step = pl.program_id(0)
    side = ratings_ref.shape[1]
    f32, bf16 = jnp.float32, jnp.bfloat16

    @pl.when(step == 0)
    def _():
        acc_ref[:, 0:2 * side, :] = jnp.zeros((acc_ref.shape[0], 2 * side, side), f32)
        if with_diag:
            acc_ref[:, 2 * side:, :] = diag_ref[...]

    count = count_ref[0]

    @pl.when(step * per_block < count)
    def _():
        for k in range(per_block):
            slot = step * per_block + k
            ub = users_ref[slot]
            ib = items_ref[slot]
            user_rows = panel_ref[ub, 0:side, :]
            item_rows = panel_ref[ib, side:2 * side, :]
            user_cols = panel_ref[ub, 2 * side:3 * side, :]
            item_cols = panel_ref[ib, 3 * side:4 * side, :]
            predicted = jnp.dot(user_rows, item_cols, preferred_element_type=f32)
            residual = (weighted_ref[k].astype(f32) * (ratings_ref[k].astype(f32) - predicted)).astype(bf16)
            acc_ref[ub, 0:side, :] += jnp.dot(residual, item_rows, preferred_element_type=f32)
            acc_ref[ib, side:2 * side, :] += jnp.dot(user_cols, residual, preferred_element_type=f32)


def tile_terms(blocks, count, tile_users, tile_items, panel, ratings, weighted, diag=None):
    with_diag = diag is not None
    slots, side, _ = ratings.shape
    per_block = PER_BLOCK
    grid = slots // per_block
    acc_rows = 2 * side + (diag.shape[1] if with_diag else 0)

    def tile_map(step, count_ref, *_):
        last = jnp.maximum((count_ref[0] - 1) // per_block, 0)
        return (jnp.minimum(step, last), 0, 0)

    def whole(step, *_):
        return (0, 0, 0)

    in_specs = [
        pl.BlockSpec(panel.shape, whole),
        pl.BlockSpec((per_block, side, side), tile_map),
        pl.BlockSpec((per_block, side, side), tile_map),
    ]
    operands = [panel, ratings, weighted]
    if with_diag:
        in_specs.append(pl.BlockSpec(diag.shape, whole))
        operands.append(diag)
    flops = slots * (3 * 2 * side * side * side)
    bytes_accessed = 2 * ratings.size * 2 + panel.size * 2 + blocks * acc_rows * side * 4
    return pl.pallas_call(
        functools.partial(tile_kernel, with_diag, per_block),
        out_shape=jax.ShapeDtypeStruct((blocks, acc_rows, side), jnp.float32),
        grid_spec=pltpu.PrefetchScalarGridSpec(
            num_scalar_prefetch=3,
            grid=(grid,),
            in_specs=in_specs,
            out_specs=pl.BlockSpec((blocks, acc_rows, side), whole),
        ),
        compiler_params=pltpu.CompilerParams(dimension_semantics=("arbitrary",)),
        cost_estimate=pl.CostEstimate(flops=flops, bytes_accessed=bytes_accessed, transcendentals=0),
    )(count, tile_users, tile_items, *operands)


def prepare(weights, row_masks, tile_users, tile_items, tile_counts, blocks):
    f32 = jnp.float32
    slots, side, _ = weights.shape
    lanes = jnp.arange(side, dtype=jnp.int32)
    bits = jnp.bitwise_and(jnp.right_shift(row_masks[:, lanes // 32], lanes % 32), 1)
    live = (jnp.arange(slots, dtype=jnp.int32) < tile_counts[0]).astype(f32)
    keep = bits.astype(f32) * live[:, None]
    weighted = weights.astype(f32) * keep[:, :, None]
    row_sums = jnp.sum(weighted, axis=2)
    col_sums = jnp.sum(weighted, axis=1)
    ids = jnp.arange(blocks, dtype=jnp.int32)[:, None]
    user_hot = (tile_users[None, :] == ids).astype(f32)
    item_hot = (tile_items[None, :] == ids).astype(f32)
    user_diag = jnp.dot(user_hot, row_sums, precision=lax.Precision.HIGHEST)
    item_diag = jnp.dot(item_hot, col_sums, precision=lax.Precision.HIGHEST)
    diag = jnp.concatenate([user_diag[:, None], item_diag[:, None], jnp.zeros((blocks, 6, side), f32)], axis=1)
    return weighted.astype(jnp.bfloat16), diag


def gather_panel(users, items, blocks):
    own = jnp.concatenate([users.astype(jnp.bfloat16), items.astype(jnp.bfloat16)], axis=0)
    copies = jnp.broadcast_to(own[None], (blocks,) + own.shape)
    gathered = lax.all_to_all(copies, "item", 0, 0, tiled=False)
    return jnp.concatenate([gathered, jnp.swapaxes(gathered[:, :users.shape[0]], 1, 2),
                            jnp.swapaxes(gathered[:, users.shape[0]:], 1, 2)], axis=1)


def sum_over_user(part, groups):
    assert groups & (groups - 1) == 0
    distance = 1
    while distance < groups:
        pairs = [(j, j ^ distance) for j in range(groups)]
        part = part + lax.ppermute(part, "user", pairs)
        distance *= 2
    return part


def on_device(groups, blocks, ratings, weights, row_masks, tile_users, tile_items, tile_counts, users, items):
    side = ratings.shape[1]
    weighted, diag = prepare(weights, row_masks, tile_users, tile_items, tile_counts, blocks)
    user_weight = None
    item_weight = None
    for iteration in range(STEPS):
        with_diag = iteration == 0
        panel = gather_panel(users, items, blocks)
        acc = tile_terms(blocks, tile_counts, tile_users, tile_items, panel, ratings, weighted,
                         diag if with_diag else None)
        total = jnp.sum(lax.all_to_all(acc, "item", 0, 0, tiled=False), axis=0)
        item_total = sum_over_user(total[side:], groups)
        user_grad = total[0:side]
        item_grad = item_total[0:side].T
        if with_diag:
            user_weight = 2.0 * side + total[2 * side]
            item_weight = 2.0 * side + item_total[side + 1]
        users = users + STEP_SCALE * (user_grad / user_weight[:, None] - DECAY_RATE * users)
        items = items + STEP_SCALE * (item_grad / item_weight[:, None] - DECAY_RATE * items)
    return (users, items)


def solution(mesh):
    groups = mesh.shape["user"]
    blocks = mesh.shape["item"]
    return jax.shard_map(
        functools.partial(on_device, groups, blocks),
        mesh=mesh,
        in_specs=(
            P(("user", "item"), None, None),
            P(("user", "item"), None, None),
            P(("user", "item"), None),
            P(("user", "item")),
            P(("user", "item")),
            P(("user", "item")),
            P(("user", "item"), None),
            P("item", None),
        ),
        out_specs=(P(("user", "item"), None), P("item", None)),
        check_vma=False,
    )
```

time: 200 us -> 198 us (0.990)
  waiting for transfers between devices: 35.7 us -> 24 us
  blocking collectives: 104 us -> 95.7 us
  other arithmetic: 5.11 us -> 13.3 us
  Pallas kernels: 16.9 us -> 23.3 us
    all_to_all x1, waiting for transfers between devices: 14.3 us -> 5.77 us  [gather_panel(): gathered = lax.all_to_all(copies, 'item', 0, 0, tiled=False)]
    all_to_all x2, blocking collectives: 86.8 us -> 78.6 us  [on_device(): total = jnp.sum(lax.all_to_all(acc, 'item', 0, 0, tiled=False), axis=0)]
    reduce_sum x0 -> x1, other arithmetic: none -> 7.38 us  [prepare(): row_sums = jnp.sum(weighted, axis=2)]
    pallas_call x2, Pallas kernels: 16.9 us -> 23.3 us  [tile_terms(): pl.pallas_call(functools.partial(tile_kernel, with_diag, per_block), out_...]
    ppermute x8, waiting for transfers between devices: 21.3 us -> 18.3 us  [sum_over_user(): part = part + lax.ppermute(part, 'user', pairs)]
  transfers between devices with their start and end apart: 9 -> 9, of which waited for: 9 -> 9; matrix products, arithmetic and copies ran while one was open for 1% -> 5% of each run, Pallas kernels for 0% -> 0%
where the time goes in v4:
time: 198 us; the launch traced here: 197 us
  blocking collectives  95.7 us (48%)
  starting transfers between devices  32.8 us (17%)
  waiting for transfers between devices  24 us (12%)
  Pallas kernels  23.3 us (12%)
  other arithmetic  13.3 us (7%)
  local copies, waits for them, and re-layouts  5.83 us (3%)
    all_to_all x2, blocking collectives, on_device(): total = jnp.sum(lax.all_to_all(acc, 'item', 0, 0, tiled=False), axis=0)  78.6 us
    ppermute x8, starting transfers between devices, sum_over_user(): part = part + lax.ppermute(part, 'user', pairs)  25.4 us
    pallas_call x2, Pallas kernels, tile_terms(): pl.pallas_call(functools.partial(tile_kernel, with_diag, per_block), out_...  23.3 us
    ppermute x8, waiting for transfers between devices, sum_over_user(): part = part + lax.ppermute(part, 'user', pairs)  18.3 us
    all_to_all x1, blocking collectives, gather_panel(): gathered = lax.all_to_all(copies, 'item', 0, 0, tiled=False)  17.1 us
    all_to_all x1, starting transfers between devices, gather_panel(): gathered = lax.all_to_all(copies, 'item', 0, 0, tiled=False)  7.48 us
    reduce_sum x1, other arithmetic, prepare(): row_sums = jnp.sum(weighted, axis=2)  7.38 us
    all_to_all x1, waiting for transfers between devices, gather_panel(): gathered = lax.all_to_all(copies, 'item', 0, 0, tiled=False)  5.77 us
  transfers between devices with their start and end apart: 9, of which 9 were waited for; matrix products, arithmetic and copies ran while one was open for 5% of the time, Pallas kernels for 0%

profile of v4, /device:TPU:2, one launch (start us, length us, event | category | flops | bytes accessed | tf_op | source)
XLA Modules:
  0.0 196.8 jit_solution(2566127449788586928)
XLA Ops:
  0.6 0.0 copy-start
  0.6 0.9 convert_element_type.34
  1.5 0.8 convert_element_type.35
  2.3 0.1 copy.24
  2.5 1.1 broadcast_in_dim.10
  3.5 7.5 %all-to-all-start = ((bf16[16,256,128]{1,2,0:T(8,128)(2,1)}), bf16[16,256,128]{1,2,0:T(8,128)(2,1)S(1)}, u32[]{:S(2)}, u32[]{:S(2)}) async-start(bf16[16,256,128]{1,2,0:T(8,128)(2,1)} %broadcast_in_dim.10), calls=%async_computation | async-start | bytes 2097152 | tf_op jit(solution)/shard_map/all_to_all | solution.py:113
  11.7 0.0 copy-done
  11.7 0.6 gather_fusion
  12.4 0.1 multiply_bitcast_fusion
  12.5 0.1 copy.26
  12.6 0.1 pad.7.clone
  12.6 0.0 copy-start.3
  12.6 0.0 copy-start.4
  12.6 7.4 %fusion.1 = (f32[120,128]{1,0:T(8,128)S(1)}, f32[120,128]{1,0:T(8,128)S(1)}, bf16[120,128,128]{2,1,0:T(8,128)(2,1)}) fusion(bf16[120,128,128]{2,1,0:T(8,128)(2,1)} %param.9, f32[120,128]{1,0:T(8,128)S(1)} %copy.26), kind=kLoop, calls=%fused_computation.3 | loop fusion | flops 9799680 | bytes 8048640 | tf_op jit(solution)/shard_map/reduce_sum | solution.py:99
  20.0 0.0 copy-done.3
  20.0 0.1 fusion.9
  20.2 0.0 copy-done.4
  20.2 0.2 fusion.10
  20.3 0.7 maximum_maximum_fusion.refs_3_
  21.0 5.8 %all-to-all-done = bf16[16,256,128]{1,2,0:T(8,128)(2,1)S(1)} async-done(((bf16[16,256,128]{1,2,0:T(8,128)(2,1)}), bf16[16,256,128]{1,2,0:T(8,128)(2,1)S(1)}, u32[]{:S(2)}, u32[]{:S(2)}) %all-to-all-start) | async-done | bytes 1048608 | tf_op jit(solution)/shard_map/all_to_all | solution.py:113
  26.8 0.3 slice_bitcast_fusion.3
  27.1 0.7 copy.25
  27.8 1.5 pad_maximum_fusion.refs_0_
  29.3 11.7 %shard_map.95 = f32[16,264,128]{2,1,0:T(8,128)} custom-call(s32[1]{0:T(128)} %copy.38.count_ref, s32[120]{0:T(128)} %users_ref.3, s32[120]{0:T(128)} %items_ref.3, bf16[16,512,128]{2,1,0:T(8,128)(2,1)} %pad_maximum_fusion.refs_0_, bf16[120,128,128]{2,1,0:T(8,128)(2,1)} %refs_1_.3, bf16[120,128,128]{2,1,0:T(8,128)(2,1)} %get-tuple-element.6.refs_2_, ...), custom_call_target="tpu_custom_call" | custom-call | flops 1509949440 | bytes 12124160 | tf_op jit(solution)/shard_map/pallas_call | solution.py:77
  40.9 0.0 copy-start.1
  40.9 0.0 copy-start.2
  40.9 41.3 %all_to_all.20 = f32[16,264,128]{2,1,0:T(8,128)S(1)} all-to-all(f32[16,264,128]{2,1,0:T(8,128)} %shard_map.95), channel_id=1, replica_groups=mesh['user'=16,'item'=16] {'item'}, dimensions={0} | all-to-all | bytes 4325376 | tf_op jit(solution)/shard_map/all_to_all | solution.py:138
  82.2 0.1 reduce_sum.38
  82.3 0.1 collective-permute-start
  82.4 1.2 collective-permute-done
  83.7 3.7 %collective-permute-start.1 = (f32[136,128]{1,0:T(8,128)S(1)}, f32[136,128]{1,0:T(8,128)S(1)}, u32[]{:S(2)}, u32[]{:S(2)}) collective-permute-start(f32[136,128]{1,0:T(8,128)S(1)} %slice_add_fusion.3), channel_id=1, source_target_pairs={{0,32},{16,48},{32,0},{48,16},{64,96},{80,112},{96,64},{112,80},{1... | collective-permute-start | bytes 208904 | tf_op jit(solution)/shard_map/ppermute | solution.py:123
  87.4 0.0 copy-done.1
  87.4 0.1 copy.31
  87.5 0.0 copy-done.2
  87.5 0.1 copy.29
  87.6 2.3 %collective-permute-done.1 = f32[136,128]{1,0:T(8,128)S(1)} collective-permute-done((f32[136,128]{1,0:T(8,128)S(1)}, f32[136,128]{1,0:T(8,128)S(1)}, u32[]{:S(2)}, u32[]{:S(2)}) %collective-permute-start.1) | collective-permute-done | bytes 69664 | tf_op jit(solution)/shard_map/ppermute | solution.py:123
  89.9 3.3 %collective-permute-start.2 = (f32[136,128]{1,0:T(8,128)S(1)}, f32[136,128]{1,0:T(8,128)S(1)}, u32[]{:S(2)}, u32[]{:S(2)}) collective-permute-start(f32[136,128]{1,0:T(8,128)S(1)} %add.94), channel_id=1, source_target_pairs={{0,64},{16,80},{32,96},{48,112},{64,0},{80,16},{96,32},{112,48},{1... | collective-permute-start | bytes 208904 | tf_op jit(solution)/shard_map/ppermute | solution.py:123
  93.2 0.1 copy.36
  93.3 2.2 %collective-permute-done.2 = f32[136,128]{1,0:T(8,128)S(1)} collective-permute-done((f32[136,128]{1,0:T(8,128)S(1)}, f32[136,128]{1,0:T(8,128)S(1)}, u32[]{:S(2)}, u32[]{:S(2)}) %collective-permute-start.2) | collective-permute-done | bytes 69664 | tf_op jit(solution)/shard_map/ppermute | solution.py:123
  95.5 7.4 %collective-permute-start.3 = (f32[136,128]{1,0:T(8,128)S(1)}, f32[136,128]{1,0:T(8,128)S(1)}, u32[]{:S(2)}, u32[]{:S(2)}) collective-permute-start(f32[136,128]{1,0:T(8,128)S(1)} %add.95), channel_id=1, source_target_pairs={{0,128},{16,144},{32,160},{48,176},{64,192},{80,208},{96,224},{112... | collective-permute-start | bytes 208904 | tf_op jit(solution)/shard_map/ppermute | solution.py:123
  102.9 3.0 %collective-permute-done.3 = f32[136,128]{1,0:T(8,128)S(1)} collective-permute-done((f32[136,128]{1,0:T(8,128)S(1)}, f32[136,128]{1,0:T(8,128)S(1)}, u32[]{:S(2)}, u32[]{:S(2)}) %collective-permute-start.3) | collective-permute-done | bytes 69664 | tf_op jit(solution)/shard_map/ppermute | solution.py:123
  106.0 0.1 broadcast_in_dim.14
  106.1 17.1 %all_to_all.21 = bf16[16,256,128]{1,2,0:T(8,128)(2,1)S(1)} all-to-all(bf16[16,256,128]{1,2,0:T(8,128)(2,1)S(1)} %broadcast_in_dim.14), channel_id=1, replica_groups=mesh['user'=16,'item'=16] {'item'}, dimensions={0} | all-to-all | bytes 2097152 | tf_op jit(solution)/shard_map/all_to_all | solution.py:113
  123.2 0.3 slice_bitcast_fusion.1
  123.4 0.7 copy.32
  124.1 1.5 pad_maximum_fusion.1.refs_0_
  125.6 11.6 %shard_map.96 = f32[16,256,128]{2,1,0:T(8,128)} custom-call(s32[1]{0:T(128)} %copy.38.count_ref, s32[120]{0:T(128)} %users_ref.3, s32[120]{0:T(128)} %items_ref.3, bf16[16,512,128]{2,1,0:T(8,128)(2,1)} %pad_maximum_fusion.1.refs_0_, bf16[120,128,128]{2,1,0:T(8,128)(2,1)} %refs_1_.3, bf16[120,128,128]{2,1,0:T(8,128)(2,1)} %get-tuple-element.6.refs_2_), custom_call_target="tpu_custom_call" | custom-call | flops 1509949440 | bytes 12058624 | tf_op jit(solution)/shard_map/pallas_call | solution.py:77
  137.2 37.4 %all_to_all.22 = f32[16,256,128]{2,1,0:T(8,128)S(1)} all-to-all(f32[16,256,128]{2,1,0:T(8,128)} %shard_map.96), channel_id=1, replica_groups=mesh['user'=16,'item'=16] {'item'}, dimensions={0} | all-to-all | bytes 4194304 | tf_op jit(solution)/shard_map/all_to_all | solution.py:138
  174.6 0.1 reduce_sum.39
  174.7 0.1 collective-permute-start.4
  174.8 1.2 collective-permute-done.4
  176.1 2.7 %collective-permute-start.5 = (f32[128,128]{1,0:T(8,128)S(1)}, f32[128,128]{1,0:T(8,128)S(1)}, u32[]{:S(2)}, u32[]{:S(2)}) collective-permute-start(f32[128,128]{1,0:T(8,128)S(1)} %get-tuple-element.11), channel_id=1, source_target_pairs={{0,32},{16,48},{32,0},{48,16},{64,96},{80,112},{96,64},{112,80},{1... | collective-permute-start | bytes 196616 | tf_op jit(solution)/shard_map/ppermute | solution.py:123
  178.8 2.4 %collective-permute-done.5 = f32[128,128]{1,0:T(8,128)S(1)} collective-permute-done((f32[128,128]{1,0:T(8,128)S(1)}, f32[128,128]{1,0:T(8,128)S(1)}, u32[]{:S(2)}, u32[]{:S(2)}) %collective-permute-start.5) | collective-permute-done | bytes 65568 | tf_op jit(solution)/shard_map/ppermute | solution.py:123
  181.2 1.6 collective-permute-start.6
  182.8 0.1 copy.37
  182.9 3.7 %collective-permute-done.6 = f32[128,128]{1,0:T(8,128)S(1)} collective-permute-done((f32[128,128]{1,0:T(8,128)S(1)}, f32[128,128]{1,0:T(8,128)S(1)}, u32[]{:S(2)}, u32[]{:S(2)}) %collective-permute-start.6) | collective-permute-done | bytes 65568 | tf_op jit(solution)/shard_map/ppermute | solution.py:123
  186.6 6.6 %collective-permute-start.7 = (f32[128,128]{1,0:T(8,128)S(1)}, f32[128,128]{1,0:T(8,128)S(1)}, u32[]{:S(2)}, u32[]{:S(2)}) collective-permute-start(f32[128,128]{1,0:T(8,128)S(1)} %add.103), channel_id=1, source_target_pairs={{0,128},{16,144},{32,160},{48,176},{64,192},{80,208},{96,224},{112... | collective-permute-start | bytes 196616 | tf_op jit(solution)/shard_map/ppermute | solution.py:123
  193.1 0.7 copy.34
  193.9 2.2 %collective-permute-done.7 = f32[128,128]{1,0:T(8,128)S(1)} collective-permute-done((f32[128,128]{1,0:T(8,128)S(1)}, f32[128,128]{1,0:T(8,128)S(1)}, u32[]{:S(2)}, u32[]{:S(2)}) %collective-permute-start.7) | collective-permute-done | bytes 65568 | tf_op jit(solution)/shard_map/ppermute | solution.py:123
  196.1 0.7 copy.35
  (23 shorter events, 0.2 us)
Async XLA Ops:
  0.6 11.1 %copy-start = (s32[120,4]{0,1:T(4,128)S(1)}, s32[120,4]{0,1:T(4,128)}, u32[]{:S(2)}) copy-start(s32[120,4]{0,1:T(4,128)} %param.10) | copy-start | bytes 5764
  3.5 23.3 %all-to-all-start = ((bf16[16,256,128]{1,2,0:T(8,128)(2,1)}), bf16[16,256,128]{1,2,0:T(8,128)(2,1)S(1)}, u32[]{:S(2)}, u32[]{:S(2)}) async-start(bf16[16,256,128]{1,2,0:T(8,128)(2,1)} %broadcast_in_dim.10), calls=%async_computation | async-start | bytes 2097152 | tf_op jit(solution)/shard_map/all_to_all | solution.py:113
  12.6 7.4 %copy-start.3 = (s32[120]{0:T(128)S(1)}, s32[120]{0:T(128)}, u32[]{:S(2)}) copy-start(s32[120]{0:T(128)} %users_ref.3) | copy-start | bytes 1444
  12.6 7.5 %copy-start.4 = (s32[120]{0:T(128)S(1)}, s32[120]{0:T(128)}, u32[]{:S(2)}) copy-start(s32[120]{0:T(128)} %items_ref.3) | copy-start | bytes 1444
  40.9 46.4 %copy-start.1 = (f32[128,128]{1,0:T(8,128)S(1)}, f32[128,128]{1,0:T(8,128)}, u32[]{:S(2)}) copy-start(f32[128,128]{1,0:T(8,128)} %param.15) | copy-start | bytes 196612
  40.9 46.5 %copy-start.2 = (f32[128,128]{1,0:T(8,128)S(1)}, f32[128,128]{1,0:T(8,128)}, u32[]{:S(2)}) copy-start(f32[128,128]{1,0:T(8,128)} %param.14) | copy-start | bytes 196612
  82.3 1.3 collective-permute-start
  83.7 6.2 %collective-permute-start.1 = (f32[136,128]{1,0:T(8,128)S(1)}, f32[136,128]{1,0:T(8,128)S(1)}, u32[]{:S(2)}, u32[]{:S(2)}) collective-permute-start(f32[136,128]{1,0:T(8,128)S(1)} %slice_add_fusion.3), channel_id=1, source_target_pairs={{0,32},{16,48},{32,0},{48,16},{64,96},{80,112},{96,64},{112,80},{1... | collective-permute-start | bytes 208904 | tf_op jit(solution)/shard_map/ppermute | solution.py:123
  89.9 5.6 %collective-permute-start.2 = (f32[136,128]{1,0:T(8,128)S(1)}, f32[136,128]{1,0:T(8,128)S(1)}, u32[]{:S(2)}, u32[]{:S(2)}) collective-permute-start(f32[136,128]{1,0:T(8,128)S(1)} %add.94), channel_id=1, source_target_pairs={{0,64},{16,80},{32,96},{48,112},{64,0},{80,16},{96,32},{112,48},{1... | collective-permute-start | bytes 208904 | tf_op jit(solution)/shard_map/ppermute | solution.py:123
  95.5 10.4 %collective-permute-start.3 = (f32[136,128]{1,0:T(8,128)S(1)}, f32[136,128]{1,0:T(8,128)S(1)}, u32[]{:S(2)}, u32[]{:S(2)}) collective-permute-start(f32[136,128]{1,0:T(8,128)S(1)} %add.95), channel_id=1, source_target_pairs={{0,128},{16,144},{32,160},{48,176},{64,192},{80,208},{96,224},{112... | collective-permute-start | bytes 208904 | tf_op jit(solution)/shard_map/ppermute | solution.py:123
  174.7 1.3 collective-permute-start.4
  176.1 5.1 %collective-permute-start.5 = (f32[128,128]{1,0:T(8,128)S(1)}, f32[128,128]{1,0:T(8,128)S(1)}, u32[]{:S(2)}, u32[]{:S(2)}) collective-permute-start(f32[128,128]{1,0:T(8,128)S(1)} %get-tuple-element.11), channel_id=1, source_target_pairs={{0,32},{16,48},{32,0},{48,16},{64,96},{80,112},{96,64},{112,80},{1... | collective-permute-start | bytes 196616 | tf_op jit(solution)/shard_map/ppermute | solution.py:123
  181.2 5.3 %collective-permute-start.6 = (f32[128,128]{1,0:T(8,128)S(1)}, f32[128,128]{1,0:T(8,128)S(1)}, u32[]{:S(2)}, u32[]{:S(2)}) collective-permute-start(f32[128,128]{1,0:T(8,128)S(1)} %add.102), channel_id=1, source_target_pairs={{0,64},{16,80},{32,96},{48,112},{64,0},{80,16},{96,32},{112,48},{1... | collective-permute-start | bytes 196616 | tf_op jit(solution)/shard_map/ppermute | solution.py:123
  186.6 9.5 %collective-permute-start.7 = (f32[128,128]{1,0:T(8,128)S(1)}, f32[128,128]{1,0:T(8,128)S(1)}, u32[]{:S(2)}, u32[]{:S(2)}) collective-permute-start(f32[128,128]{1,0:T(8,128)S(1)} %add.103), channel_id=1, source_target_pairs={{0,128},{16,144},{32,160},{48,176},{64,192},{80,208},{96,224},{112... | collective-permute-start | bytes 196616 | tf_op jit(solution)/shard_map/ppermute | solution.py:123

commit v5 on v4

--- a/solution.py
+++ b/solution.py
@@ -13,14 +13,14 @@
 STEP_SCALE = 4.0
 DECAY_RATE = 0.02
 
-PER_BLOCK = 24
+PER_BLOCK = 40
 
 
 def tile_kernel(with_diag, per_block, count_ref, users_ref, items_ref, *refs):
     if with_diag:
-        panel_ref, ratings_ref, weighted_ref, diag_ref, acc_ref = refs
+        panel_ref, ratings_ref, weighted_ref, diag_ref, acc_ref, residual_ref = refs
     else:
-        panel_ref, ratings_ref, weighted_ref, acc_ref = refs
+        panel_ref, ratings_ref, weighted_ref, acc_ref, residual_ref = refs
     step = pl.program_id(0)
     side = ratings_ref.shape[1]
     f32, bf16 = jnp.float32, jnp.bfloat16
@@ -40,11 +40,16 @@
             ub = users_ref[slot]
             ib = items_ref[slot]
             user_rows = panel_ref[ub, 0:side, :]
+            item_cols = panel_ref[ib, 3 * side:4 * side, :]
+            predicted = jnp.dot(user_rows, item_cols, preferred_element_type=f32)
+            residual_ref[k] = (weighted_ref[k].astype(f32) * (ratings_ref[k].astype(f32) - predicted)).astype(bf16)
+        for k in range(per_block):
+            slot = step * per_block + k
+            ub = users_ref[slot]
+            ib = items_ref[slot]
+            residual = residual_ref[k]
             item_rows = panel_ref[ib, side:2 * side, :]
             user_cols = panel_ref[ub, 2 * side:3 * side, :]
-            item_cols = panel_ref[ib, 3 * side:4 * side, :]
-            predicted = jnp.dot(user_rows, item_cols, preferred_element_type=f32)
-            residual = (weighted_ref[k].astype(f32) * (ratings_ref[k].astype(f32) - predicted)).astype(bf16)
             acc_ref[ub, 0:side, :] += jnp.dot(residual, item_rows, preferred_element_type=f32)
             acc_ref[ib, side:2 * side, :] += jnp.dot(user_cols, residual, preferred_element_type=f32)
 
@@ -82,6 +87,7 @@
             grid=(grid,),
             in_specs=in_specs,
             out_specs=pl.BlockSpec((blocks, acc_rows, side), whole),
+            scratch_shapes=[pltpu.VMEM((per_block, side, side), jnp.bfloat16)],
         ),
         compiler_params=pltpu.CompilerParams(dimension_semantics=("arbitrary",)),
         cost_estimate=pl.CostEstimate(flops=flops, bytes_accessed=bytes_accessed, transcendentals=0),

time: 198 us -> 171 us (0.86)
  blocking collectives: 95.7 us -> 79.4 us
  Pallas kernels: 23.3 us -> 12.3 us
    all_to_all x2, blocking collectives: 78.6 us -> 62.7 us  [on_device(): total = jnp.sum(lax.all_to_all(acc, 'item', 0, 0, tiled=False), axis=0)]
    pallas_call x2, Pallas kernels: 23.3 us -> 12.3 us  [tile_terms(): pl.pallas_call(functools.partial(tile_kernel, with_diag, per_block), out_...]
  transfers between devices with their start and end apart: 9 -> 9, of which waited for: 9 -> 9; matrix products, arithmetic and copies ran while one was open for 5% -> 6% of each run, Pallas kernels for 0% -> 0%
where the time goes in v5:
time: 171 us; the launch traced here: 170 us
  blocking collectives  79.4 us (46%)
  starting transfers between devices  33.3 us (19%)
  waiting for transfers between devices  24.5 us (14%)
  other arithmetic  13.3 us (8%)
  Pallas kernels  12.3 us (7%)
  local copies, waits for them, and re-layouts  5.83 us (3%)
    all_to_all x2, blocking collectives, on_device(): total = jnp.sum(lax.all_to_all(acc, 'item', 0, 0, tiled=False), axis=0)  62.7 us
    ppermute x8, starting transfers between devices, sum_over_user(): part = part + lax.ppermute(part, 'user', pairs)  25.8 us
    ppermute x8, waiting for transfers between devices, sum_over_user(): part = part + lax.ppermute(part, 'user', pairs)  18.8 us
    all_to_all x1, blocking collectives, gather_panel(): gathered = lax.all_to_all(copies, 'item', 0, 0, tiled=False)  16.7 us
    pallas_call x2, Pallas kernels, tile_terms(): pl.pallas_call(functools.partial(tile_kernel, with_diag, per_block), out_...  12.3 us
    all_to_all x1, starting transfers between devices, gather_panel(): gathered = lax.all_to_all(copies, 'item', 0, 0, tiled=False)  7.48 us
    reduce_sum x1, other arithmetic, prepare(): row_sums = jnp.sum(weighted, axis=2)  7.38 us
    all_to_all x1, waiting for transfers between devices, gather_panel(): gathered = lax.all_to_all(copies, 'item', 0, 0, tiled=False)  5.77 us
  transfers between devices with their start and end apart: 9, of which 9 were waited for; matrix products, arithmetic and copies ran while one was open for 6% of the time, Pallas kernels for 0%

profile of v5, /device:TPU:2, one launch (start us, length us, event | category | flops | bytes accessed | tf_op | source)
XLA Modules:
  0.0 170.5 jit_solution(6876256198791817212)
XLA Ops:
  0.6 0.0 copy-start
  0.6 0.9 convert_element_type.34
  1.5 0.8 convert_element_type.35
  2.3 0.1 copy.24
  2.5 1.1 broadcast_in_dim.10
  3.5 7.5 %all-to-all-start = ((bf16[16,256,128]{1,2,0:T(8,128)(2,1)}), bf16[16,256,128]{1,2,0:T(8,128)(2,1)S(1)}, u32[]{:S(2)}, u32[]{:S(2)}) async-start(bf16[16,256,128]{1,2,0:T(8,128)(2,1)} %broadcast_in_dim.10), calls=%async_computation | async-start | bytes 2097152 | tf_op jit(solution)/shard_map/all_to_all | solution.py:119
  11.7 0.0 copy-done
  11.7 0.6 gather_fusion
  12.4 0.1 multiply_bitcast_fusion
  12.5 0.1 copy.26
  12.6 0.1 pad.7.clone
  12.6 0.0 copy-start.3
  12.6 0.0 copy-start.4
  12.6 7.4 %fusion.1 = (f32[120,128]{1,0:T(8,128)S(1)}, f32[120,128]{1,0:T(8,128)S(1)}, bf16[120,128,128]{2,1,0:T(8,128)(2,1)}) fusion(bf16[120,128,128]{2,1,0:T(8,128)(2,1)} %param.9, f32[120,128]{1,0:T(8,128)S(1)} %copy.26), kind=kLoop, calls=%fused_computation.3 | loop fusion | flops 9799680 | bytes 8048640 | tf_op jit(solution)/shard_map/reduce_sum | solution.py:105
  20.0 0.0 copy-done.3
  20.0 0.1 fusion.9
  20.2 0.0 copy-done.4
  20.2 0.2 fusion.10
  20.3 0.7 maximum_maximum_fusion.refs_3_
  21.0 5.8 %all-to-all-done = bf16[16,256,128]{1,2,0:T(8,128)(2,1)S(1)} async-done(((bf16[16,256,128]{1,2,0:T(8,128)(2,1)}), bf16[16,256,128]{1,2,0:T(8,128)(2,1)S(1)}, u32[]{:S(2)}, u32[]{:S(2)}) %all-to-all-start) | async-done | bytes 1048608 | tf_op jit(solution)/shard_map/all_to_all | solution.py:119
  26.8 0.3 slice_bitcast_fusion.3
  27.1 0.7 copy.25
  27.8 1.5 pad_maximum_fusion.refs_0_
  29.3 6.2 %shard_map.95 = f32[16,264,128]{2,1,0:T(8,128)} custom-call(s32[1]{0:T(128)} %copy.38.count_ref, s32[120]{0:T(128)} %users_ref.3, s32[120]{0:T(128)} %items_ref.3, bf16[16,512,128]{2,1,0:T(8,128)(2,1)} %pad_maximum_fusion.refs_0_, bf16[120,128,128]{2,1,0:T(8,128)(2,1)} %refs_1_.3, bf16[120,128,128]{2,1,0:T(8,128)(2,1)} %get-tuple-element.6.refs_2_, ...), custom_call_target="tpu_custom_call" | custom-call | flops 1509949440 | bytes 12124160 | tf_op jit(solution)/shard_map/pallas_call | solution.py:82
  35.5 0.0 copy-start.1
  35.5 0.0 copy-start.2
  35.5 33.4 %all_to_all.20 = f32[16,264,128]{2,1,0:T(8,128)S(1)} all-to-all(f32[16,264,128]{2,1,0:T(8,128)} %shard_map.95), channel_id=1, replica_groups=mesh['user'=16,'item'=16] {'item'}, dimensions={0} | all-to-all | bytes 4325376 | tf_op jit(solution)/shard_map/all_to_all | solution.py:144
  68.8 0.1 reduce_sum.38
  68.9 0.1 collective-permute-start
  69.0 1.2 collective-permute-done
  70.3 2.5 %collective-permute-start.1 = (f32[136,128]{1,0:T(8,128)S(1)}, f32[136,128]{1,0:T(8,128)S(1)}, u32[]{:S(2)}, u32[]{:S(2)}) collective-permute-start(f32[136,128]{1,0:T(8,128)S(1)} %slice_add_fusion.3), channel_id=1, source_target_pairs={{0,32},{16,48},{32,0},{48,16},{64,96},{80,112},{96,64},{112,80},{1... | collective-permute-start | bytes 208904 | tf_op jit(solution)/shard_map/ppermute | solution.py:129
  72.8 0.0 copy-done.1
  72.8 0.1 copy.31
  72.9 0.0 copy-done.2
  72.9 0.1 copy.29
  73.0 2.3 %collective-permute-done.1 = f32[136,128]{1,0:T(8,128)S(1)} collective-permute-done((f32[136,128]{1,0:T(8,128)S(1)}, f32[136,128]{1,0:T(8,128)S(1)}, u32[]{:S(2)}, u32[]{:S(2)}) %collective-permute-start.1) | collective-permute-done | bytes 69664 | tf_op jit(solution)/shard_map/ppermute | solution.py:129
  75.3 4.8 %collective-permute-start.2 = (f32[136,128]{1,0:T(8,128)S(1)}, f32[136,128]{1,0:T(8,128)S(1)}, u32[]{:S(2)}, u32[]{:S(2)}) collective-permute-start(f32[136,128]{1,0:T(8,128)S(1)} %add.94), channel_id=1, source_target_pairs={{0,64},{16,80},{32,96},{48,112},{64,0},{80,16},{96,32},{112,48},{1... | collective-permute-start | bytes 208904 | tf_op jit(solution)/shard_map/ppermute | solution.py:129
  80.1 0.1 copy.36
  80.2 2.9 %collective-permute-done.2 = f32[136,128]{1,0:T(8,128)S(1)} collective-permute-done((f32[136,128]{1,0:T(8,128)S(1)}, f32[136,128]{1,0:T(8,128)S(1)}, u32[]{:S(2)}, u32[]{:S(2)}) %collective-permute-start.2) | collective-permute-done | bytes 69664 | tf_op jit(solution)/shard_map/ppermute | solution.py:129
  83.1 7.0 %collective-permute-start.3 = (f32[136,128]{1,0:T(8,128)S(1)}, f32[136,128]{1,0:T(8,128)S(1)}, u32[]{:S(2)}, u32[]{:S(2)}) collective-permute-start(f32[136,128]{1,0:T(8,128)S(1)} %add.95), channel_id=1, source_target_pairs={{0,128},{16,144},{32,160},{48,176},{64,192},{80,208},{96,224},{112... | collective-permute-start | bytes 208904 | tf_op jit(solution)/shard_map/ppermute | solution.py:129
  90.2 3.0 %collective-permute-done.3 = f32[136,128]{1,0:T(8,128)S(1)} collective-permute-done((f32[136,128]{1,0:T(8,128)S(1)}, f32[136,128]{1,0:T(8,128)S(1)}, u32[]{:S(2)}, u32[]{:S(2)}) %collective-permute-start.3) | collective-permute-done | bytes 69664 | tf_op jit(solution)/shard_map/ppermute | solution.py:129
  93.2 0.1 broadcast_in_dim.14
  93.3 16.7 %all_to_all.21 = bf16[16,256,128]{1,2,0:T(8,128)(2,1)S(1)} all-to-all(bf16[16,256,128]{1,2,0:T(8,128)(2,1)S(1)} %broadcast_in_dim.14), channel_id=1, replica_groups=mesh['user'=16,'item'=16] {'item'}, dimensions={0} | all-to-all | bytes 2097152 | tf_op jit(solution)/shard_map/all_to_all | solution.py:119
  110.1 0.3 slice_bitcast_fusion.1
  110.4 0.7 copy.32
  111.0 1.5 pad_maximum_fusion.1.refs_0_
  112.5 6.1 %shard_map.96 = f32[16,256,128]{2,1,0:T(8,128)} custom-call(s32[1]{0:T(128)} %copy.38.count_ref, s32[120]{0:T(128)} %users_ref.3, s32[120]{0:T(128)} %items_ref.3, bf16[16,512,128]{2,1,0:T(8,128)(2,1)} %pad_maximum_fusion.1.refs_0_, bf16[120,128,128]{2,1,0:T(8,128)(2,1)} %refs_1_.3, bf16[120,128,128]{2,1,0:T(8,128)(2,1)} %get-tuple-element.6.refs_2_), custom_call_target="tpu_custom_call" | custom-call | flops 1509949440 | bytes 12058624 | tf_op jit(solution)/shard_map/pallas_call | solution.py:82
  118.7 29.3 %all_to_all.22 = f32[16,256,128]{2,1,0:T(8,128)S(1)} all-to-all(f32[16,256,128]{2,1,0:T(8,128)} %shard_map.96), channel_id=1, replica_groups=mesh['user'=16,'item'=16] {'item'}, dimensions={0} | all-to-all | bytes 4194304 | tf_op jit(solution)/shard_map/all_to_all | solution.py:144
  148.0 0.1 reduce_sum.39
  148.1 0.1 collective-permute-start.4
  148.2 1.2 collective-permute-done.4
  149.5 1.2 collective-permute-start.5
  150.7 3.1 %collective-permute-done.5 = f32[128,128]{1,0:T(8,128)S(1)} collective-permute-done((f32[128,128]{1,0:T(8,128)S(1)}, f32[128,128]{1,0:T(8,128)S(1)}, u32[]{:S(2)}, u32[]{:S(2)}) %collective-permute-start.5) | collective-permute-done | bytes 65568 | tf_op jit(solution)/shard_map/ppermute | solution.py:129
  153.8 3.7 %collective-permute-start.6 = (f32[128,128]{1,0:T(8,128)S(1)}, f32[128,128]{1,0:T(8,128)S(1)}, u32[]{:S(2)}, u32[]{:S(2)}) collective-permute-start(f32[128,128]{1,0:T(8,128)S(1)} %add.102), channel_id=1, source_target_pairs={{0,64},{16,80},{32,96},{48,112},{64,0},{80,16},{96,32},{112,48},{1... | collective-permute-start | bytes 196616 | tf_op jit(solution)/shard_map/ppermute | solution.py:129
  157.5 0.1 copy.37
  157.6 2.8 %collective-permute-done.6 = f32[128,128]{1,0:T(8,128)S(1)} collective-permute-done((f32[128,128]{1,0:T(8,128)S(1)}, f32[128,128]{1,0:T(8,128)S(1)}, u32[]{:S(2)}, u32[]{:S(2)}) %collective-permute-start.6) | collective-permute-done | bytes 65568 | tf_op jit(solution)/shard_map/ppermute | solution.py:129
  160.4 6.4 %collective-permute-start.7 = (f32[128,128]{1,0:T(8,128)S(1)}, f32[128,128]{1,0:T(8,128)S(1)}, u32[]{:S(2)}, u32[]{:S(2)}) collective-permute-start(f32[128,128]{1,0:T(8,128)S(1)} %add.103), channel_id=1, source_target_pairs={{0,128},{16,144},{32,160},{48,176},{64,192},{80,208},{96,224},{112... | collective-permute-start | bytes 196616 | tf_op jit(solution)/shard_map/ppermute | solution.py:129
  166.8 0.7 copy.34
  167.5 2.2 %collective-permute-done.7 = f32[128,128]{1,0:T(8,128)S(1)} collective-permute-done((f32[128,128]{1,0:T(8,128)S(1)}, f32[128,128]{1,0:T(8,128)S(1)}, u32[]{:S(2)}, u32[]{:S(2)}) %collective-permute-start.7) | collective-permute-done | bytes 65568 | tf_op jit(solution)/shard_map/ppermute | solution.py:129
  169.8 0.7 copy.35
  (23 shorter events, 0.2 us)
Async XLA Ops:
  0.6 11.1 %copy-start = (s32[120,4]{0,1:T(4,128)S(1)}, s32[120,4]{0,1:T(4,128)}, u32[]{:S(2)}) copy-start(s32[120,4]{0,1:T(4,128)} %param.10) | copy-start | bytes 5764
  3.5 23.3 %all-to-all-start = ((bf16[16,256,128]{1,2,0:T(8,128)(2,1)}), bf16[16,256,128]{1,2,0:T(8,128)(2,1)S(1)}, u32[]{:S(2)}, u32[]{:S(2)}) async-start(bf16[16,256,128]{1,2,0:T(8,128)(2,1)} %broadcast_in_dim.10), calls=%async_computation | async-start | bytes 2097152 | tf_op jit(solution)/shard_map/all_to_all | solution.py:119
  12.6 7.4 %copy-start.3 = (s32[120]{0:T(128)S(1)}, s32[120]{0:T(128)}, u32[]{:S(2)}) copy-start(s32[120]{0:T(128)} %users_ref.3) | copy-start | bytes 1444
  12.6 7.5 %copy-start.4 = (s32[120]{0:T(128)S(1)}, s32[120]{0:T(128)}, u32[]{:S(2)}) copy-start(s32[120]{0:T(128)} %items_ref.3) | copy-start | bytes 1444
  35.5 37.3 %copy-start.1 = (f32[128,128]{1,0:T(8,128)S(1)}, f32[128,128]{1,0:T(8,128)}, u32[]{:S(2)}) copy-start(f32[128,128]{1,0:T(8,128)} %param.15) | copy-start | bytes 196612
  35.5 37.4 %copy-start.2 = (f32[128,128]{1,0:T(8,128)S(1)}, f32[128,128]{1,0:T(8,128)}, u32[]{:S(2)}) copy-start(f32[128,128]{1,0:T(8,128)} %param.14) | copy-start | bytes 196612
  68.9 1.3 collective-permute-start
  70.3 5.0 %collective-permute-start.1 = (f32[136,128]{1,0:T(8,128)S(1)}, f32[136,128]{1,0:T(8,128)S(1)}, u32[]{:S(2)}, u32[]{:S(2)}) collective-permute-start(f32[136,128]{1,0:T(8,128)S(1)} %slice_add_fusion.3), channel_id=1, source_target_pairs={{0,32},{16,48},{32,0},{48,16},{64,96},{80,112},{96,64},{112,80},{1... | collective-permute-start | bytes 208904 | tf_op jit(solution)/shard_map/ppermute | solution.py:129
  75.3 7.8 %collective-permute-start.2 = (f32[136,128]{1,0:T(8,128)S(1)}, f32[136,128]{1,0:T(8,128)S(1)}, u32[]{:S(2)}, u32[]{:S(2)}) collective-permute-start(f32[136,128]{1,0:T(8,128)S(1)} %add.94), channel_id=1, source_target_pairs={{0,64},{16,80},{32,96},{48,112},{64,0},{80,16},{96,32},{112,48},{1... | collective-permute-start | bytes 208904 | tf_op jit(solution)/shard_map/ppermute | solution.py:129
  83.1 10.0 %collective-permute-start.3 = (f32[136,128]{1,0:T(8,128)S(1)}, f32[136,128]{1,0:T(8,128)S(1)}, u32[]{:S(2)}, u32[]{:S(2)}) collective-permute-start(f32[136,128]{1,0:T(8,128)S(1)} %add.95), channel_id=1, source_target_pairs={{0,128},{16,144},{32,160},{48,176},{64,192},{80,208},{96,224},{112... | collective-permute-start | bytes 208904 | tf_op jit(solution)/shard_map/ppermute | solution.py:129
  148.1 1.3 collective-permute-start.4
  149.5 4.4 %collective-permute-start.5 = (f32[128,128]{1,0:T(8,128)S(1)}, f32[128,128]{1,0:T(8,128)S(1)}, u32[]{:S(2)}, u32[]{:S(2)}) collective-permute-start(f32[128,128]{1,0:T(8,128)S(1)} %get-tuple-element.11), channel_id=1, source_target_pairs={{0,32},{16,48},{32,0},{48,16},{64,96},{80,112},{96,64},{112,80},{1... | collective-permute-start | bytes 196616 | tf_op jit(solution)/shard_map/ppermute | solution.py:129
  153.8 6.5 %collective-permute-start.6 = (f32[128,128]{1,0:T(8,128)S(1)}, f32[128,128]{1,0:T(8,128)S(1)}, u32[]{:S(2)}, u32[]{:S(2)}) collective-permute-start(f32[128,128]{1,0:T(8,128)S(1)} %add.102), channel_id=1, source_target_pairs={{0,64},{16,80},{32,96},{48,112},{64,0},{80,16},{96,32},{112,48},{1... | collective-permute-start | bytes 196616 | tf_op jit(solution)/shard_map/ppermute | solution.py:129
  160.4 9.3 %collective-permute-start.7 = (f32[128,128]{1,0:T(8,128)S(1)}, f32[128,128]{1,0:T(8,128)S(1)}, u32[]{:S(2)}, u32[]{:S(2)}) collective-permute-start(f32[128,128]{1,0:T(8,128)S(1)} %add.103), channel_id=1, source_target_pairs={{0,128},{16,144},{32,160},{48,176},{64,192},{80,208},{96,224},{112... | collective-permute-start | bytes 196616 | tf_op jit(solution)/shard_map/ppermute | solution.py:129

commit v6 on v5

--- a/solution.py
+++ b/solution.py
@@ -121,13 +121,28 @@
                             jnp.swapaxes(gathered[:, users.shape[0]:], 1, 2)], axis=1)
 
 
+def user_rounds(groups):
+    rounds = []
+    distance = 1
+    while distance < groups:
+        rounds.append([j ^ distance for j in range(groups)])
+        distance *= 2
+    if groups != 16:
+        return rounds
+
+    def across(j):
+        z = j // 2
+        far = (6 - z) % 8 if z % 2 == 0 else (8 - z) % 8
+        return far * 2 + j % 2
+
+    return [rounds[0], rounds[2], [across(j) for j in range(groups)], rounds[1]]
+
+
 def sum_over_user(part, groups):
     assert groups & (groups - 1) == 0
-    distance = 1
-    while distance < groups:
-        pairs = [(j, j ^ distance) for j in range(groups)]
+    for partner in user_rounds(groups):
+        pairs = [(j, partner[j]) for j in range(groups)]
         part = part + lax.ppermute(part, "user", pairs)
-        distance *= 2
     return part
 
 

time: 171 us -> 172 us (level)
  blocking collectives: 79.4 us -> 85.2 us
  starting transfers between devices: 33.3 us -> 28 us
    ppermute x8, starting transfers between devices: 25.8 us -> 20.5 us  [sum_over_user(): part = part + lax.ppermute(part, 'user', pairs)]
    all_to_all x2, blocking collectives: 62.7 us -> 66.7 us  [on_device(): total = jnp.sum(lax.all_to_all(acc, 'item', 0, 0, tiled=False), axis=0)]
where the time goes in v6:
time: 172 us
  blocking collectives  85.2 us (50%)
  starting transfers between devices  28 us (16%)
  waiting for transfers between devices  25 us (15%)
  other arithmetic  13.3 us (8%)
  Pallas kernels  12.3 us (7%)
  local copies, waits for them, and re-layouts  5.83 us (3%)
    all_to_all x2, blocking collectives, on_device(): total = jnp.sum(lax.all_to_all(acc, 'item', 0, 0, tiled=False), axis=0)  66.7 us
    ppermute x8, starting transfers between devices, sum_over_user(): part = part + lax.ppermute(part, 'user', pairs)  20.5 us
    ppermute x8, waiting for transfers between devices, sum_over_user(): part = part + lax.ppermute(part, 'user', pairs)  19.3 us
    all_to_all x1, blocking collectives, gather_panel(): gathered = lax.all_to_all(copies, 'item', 0, 0, tiled=False)  18.4 us
    pallas_call x2, Pallas kernels, tile_terms(): pl.pallas_call(functools.partial(tile_kernel, with_diag, per_block), out_...  12.3 us
    all_to_all x1, starting transfers between devices, gather_panel(): gathered = lax.all_to_all(copies, 'item', 0, 0, tiled=False)  7.48 us
    reduce_sum x1, other arithmetic, prepare(): row_sums = jnp.sum(weighted, axis=2)  7.38 us
    all_to_all x1, waiting for transfers between devices, gather_panel(): gathered = lax.all_to_all(copies, 'item', 0, 0, tiled=False)  5.77 us
  transfers between devices with their start and end apart: 9, of which 9 were waited for; matrix products, arithmetic and copies ran while one was open for 6% of the time, Pallas kernels for 0%

profile of v6, /device:TPU:2, one launch (start us, length us, event | category | flops | bytes accessed | tf_op | source)
XLA Modules:
  0.0 171.5 jit_solution(11058434004695878964)
XLA Ops:
  0.6 0.0 copy-start
  0.6 0.9 convert_element_type.34
  1.5 0.8 convert_element_type.35
  2.3 0.1 copy.24
  2.5 1.1 broadcast_in_dim.10
  3.5 7.5 %all-to-all-start = ((bf16[16,256,128]{1,2,0:T(8,128)(2,1)}), bf16[16,256,128]{1,2,0:T(8,128)(2,1)S(1)}, u32[]{:S(2)}, u32[]{:S(2)}) async-start(bf16[16,256,128]{1,2,0:T(8,128)(2,1)} %broadcast_in_dim.10), calls=%async_computation | async-start | bytes 2097152 | tf_op jit(solution)/shard_map/all_to_all | solution.py:119
  11.7 0.0 copy-done
  11.7 0.6 gather_fusion
  12.4 0.1 multiply_bitcast_fusion
  12.5 0.1 copy.26
  12.6 0.1 pad.7.clone
  12.6 0.0 copy-start.3
  12.6 0.0 copy-start.4
  12.6 7.4 %fusion.1 = (f32[120,128]{1,0:T(8,128)S(1)}, f32[120,128]{1,0:T(8,128)S(1)}, bf16[120,128,128]{2,1,0:T(8,128)(2,1)}) fusion(bf16[120,128,128]{2,1,0:T(8,128)(2,1)} %param.9, f32[120,128]{1,0:T(8,128)S(1)} %copy.26), kind=kLoop, calls=%fused_computation.3 | loop fusion | flops 9799680 | bytes 8048640 | tf_op jit(solution)/shard_map/reduce_sum | solution.py:105
  20.0 0.0 copy-done.3
  20.0 0.1 fusion.9
  20.2 0.0 copy-done.4
  20.2 0.2 fusion.10
  20.3 0.7 maximum_maximum_fusion.refs_3_
  21.0 5.8 %all-to-all-done = bf16[16,256,128]{1,2,0:T(8,128)(2,1)S(1)} async-done(((bf16[16,256,128]{1,2,0:T(8,128)(2,1)}), bf16[16,256,128]{1,2,0:T(8,128)(2,1)S(1)}, u32[]{:S(2)}, u32[]{:S(2)}) %all-to-all-start) | async-done | bytes 1048608 | tf_op jit(solution)/shard_map/all_to_all | solution.py:119
  26.8 0.3 slice_bitcast_fusion.3
  27.1 0.7 copy.25
  27.8 1.5 pad_maximum_fusion.refs_0_
  29.3 6.2 %shard_map.95 = f32[16,264,128]{2,1,0:T(8,128)} custom-call(s32[1]{0:T(128)} %copy.38.count_ref, s32[120]{0:T(128)} %users_ref.3, s32[120]{0:T(128)} %items_ref.3, bf16[16,512,128]{2,1,0:T(8,128)(2,1)} %pad_maximum_fusion.refs_0_, bf16[120,128,128]{2,1,0:T(8,128)(2,1)} %refs_1_.3, bf16[120,128,128]{2,1,0:T(8,128)(2,1)} %get-tuple-element.6.refs_2_, ...), custom_call_target="tpu_custom_call" | custom-call | flops 1509949440 | bytes 12124160 | tf_op jit(solution)/shard_map/pallas_call | solution.py:82
  35.5 0.0 copy-start.1
  35.5 0.0 copy-start.2
  35.5 35.4 %all_to_all.20 = f32[16,264,128]{2,1,0:T(8,128)S(1)} all-to-all(f32[16,264,128]{2,1,0:T(8,128)} %shard_map.95), channel_id=1, replica_groups=mesh['user'=16,'item'=16] {'item'}, dimensions={0} | all-to-all | bytes 4325376 | tf_op jit(solution)/shard_map/all_to_all | solution.py:159
  70.8 0.1 reduce_sum.38
  71.0 0.1 collective-permute-start
  71.1 1.2 collective-permute-done
  72.3 2.8 %collective-permute-start.1 = (f32[136,128]{1,0:T(8,128)S(1)}, f32[136,128]{1,0:T(8,128)S(1)}, u32[]{:S(2)}, u32[]{:S(2)}) collective-permute-start(f32[136,128]{1,0:T(8,128)S(1)} %slice_add_fusion.3), channel_id=1, source_target_pairs={{0,64},{16,80},{32,96},{48,112},{64,0},{80,16},{96,32},{112,48},{1... | collective-permute-start | bytes 208904 | tf_op jit(solution)/shard_map/ppermute | solution.py:145
  75.1 0.0 copy-done.1
  75.1 0.1 copy.31
  75.2 0.0 copy-done.2
  75.2 0.1 copy.29
  75.3 2.3 %collective-permute-done.1 = f32[136,128]{1,0:T(8,128)S(1)} collective-permute-done((f32[136,128]{1,0:T(8,128)S(1)}, f32[136,128]{1,0:T(8,128)S(1)}, u32[]{:S(2)}, u32[]{:S(2)}) %collective-permute-start.1) | collective-permute-done | bytes 69664 | tf_op jit(solution)/shard_map/ppermute | solution.py:145
  77.6 6.0 %collective-permute-start.2 = (f32[136,128]{1,0:T(8,128)S(1)}, f32[136,128]{1,0:T(8,128)S(1)}, u32[]{:S(2)}, u32[]{:S(2)}) collective-permute-start(f32[136,128]{1,0:T(8,128)S(1)} %add.94), channel_id=1, source_target_pairs={{0,192},{16,208},{32,224},{48,240},{64,128},{80,144},{96,160},{112... | collective-permute-start | bytes 208904 | tf_op jit(solution)/shard_map/ppermute | solution.py:145
  83.6 0.1 copy.36
  83.7 2.2 %collective-permute-done.2 = f32[136,128]{1,0:T(8,128)S(1)} collective-permute-done((f32[136,128]{1,0:T(8,128)S(1)}, f32[136,128]{1,0:T(8,128)S(1)}, u32[]{:S(2)}, u32[]{:S(2)}) %collective-permute-start.2) | collective-permute-done | bytes 69664 | tf_op jit(solution)/shard_map/ppermute | solution.py:145
  85.9 1.8 %collective-permute-start.3 = (f32[136,128]{1,0:T(8,128)S(1)}, f32[136,128]{1,0:T(8,128)S(1)}, u32[]{:S(2)}, u32[]{:S(2)}) collective-permute-start(f32[136,128]{1,0:T(8,128)S(1)} %add.95), channel_id=1, source_target_pairs={{0,32},{16,48},{32,0},{48,16},{64,96},{80,112},{96,64},{112,80},{1... | collective-permute-start | bytes 208904 | tf_op jit(solution)/shard_map/ppermute | solution.py:145
  87.8 2.5 %collective-permute-done.3 = f32[136,128]{1,0:T(8,128)S(1)} collective-permute-done((f32[136,128]{1,0:T(8,128)S(1)}, f32[136,128]{1,0:T(8,128)S(1)}, u32[]{:S(2)}, u32[]{:S(2)}) %collective-permute-start.3) | collective-permute-done | bytes 69664 | tf_op jit(solution)/shard_map/ppermute | solution.py:145
  90.4 0.1 broadcast_in_dim.14
  90.5 18.4 %all_to_all.21 = bf16[16,256,128]{1,2,0:T(8,128)(2,1)S(1)} all-to-all(bf16[16,256,128]{1,2,0:T(8,128)(2,1)S(1)} %broadcast_in_dim.14), channel_id=1, replica_groups=mesh['user'=16,'item'=16] {'item'}, dimensions={0} | all-to-all | bytes 2097152 | tf_op jit(solution)/shard_map/all_to_all | solution.py:119
  108.9 0.3 slice_bitcast_fusion.1
  109.2 0.7 copy.32
  109.9 1.5 pad_maximum_fusion.1.refs_0_
  111.4 6.1 %shard_map.96 = f32[16,256,128]{2,1,0:T(8,128)} custom-call(s32[1]{0:T(128)} %copy.38.count_ref, s32[120]{0:T(128)} %users_ref.3, s32[120]{0:T(128)} %items_ref.3, bf16[16,512,128]{2,1,0:T(8,128)(2,1)} %pad_maximum_fusion.1.refs_0_, bf16[120,128,128]{2,1,0:T(8,128)(2,1)} %refs_1_.3, bf16[120,128,128]{2,1,0:T(8,128)(2,1)} %get-tuple-element.6.refs_2_), custom_call_target="tpu_custom_call" | custom-call | flops 1509949440 | bytes 12058624 | tf_op jit(solution)/shard_map/pallas_call | solution.py:82
  117.5 31.4 %all_to_all.22 = f32[16,256,128]{2,1,0:T(8,128)S(1)} all-to-all(f32[16,256,128]{2,1,0:T(8,128)} %shard_map.96), channel_id=1, replica_groups=mesh['user'=16,'item'=16] {'item'}, dimensions={0} | all-to-all | bytes 4194304 | tf_op jit(solution)/shard_map/all_to_all | solution.py:159
  148.9 0.1 reduce_sum.39
  149.0 0.1 collective-permute-start.4
  149.1 1.2 collective-permute-done.4
  150.4 7.2 %collective-permute-start.5 = (f32[128,128]{1,0:T(8,128)S(1)}, f32[128,128]{1,0:T(8,128)S(1)}, u32[]{:S(2)}, u32[]{:S(2)}) collective-permute-start(f32[128,128]{1,0:T(8,128)S(1)} %get-tuple-element.11), channel_id=1, source_target_pairs={{0,64},{16,80},{32,96},{48,112},{64,0},{80,16},{96,32},{112,48},{1... | collective-permute-start | bytes 196616 | tf_op jit(solution)/shard_map/ppermute | solution.py:145
  157.5 2.4 %collective-permute-done.5 = f32[128,128]{1,0:T(8,128)S(1)} collective-permute-done((f32[128,128]{1,0:T(8,128)S(1)}, f32[128,128]{1,0:T(8,128)S(1)}, u32[]{:S(2)}, u32[]{:S(2)}) %collective-permute-start.5) | collective-permute-done | bytes 65568 | tf_op jit(solution)/shard_map/ppermute | solution.py:145
  159.9 2.5 %collective-permute-start.6 = (f32[128,128]{1,0:T(8,128)S(1)}, f32[128,128]{1,0:T(8,128)S(1)}, u32[]{:S(2)}, u32[]{:S(2)}) collective-permute-start(f32[128,128]{1,0:T(8,128)S(1)} %add.102), channel_id=1, source_target_pairs={{0,192},{16,208},{32,224},{48,240},{64,128},{80,144},{96,160},{112... | collective-permute-start | bytes 196616 | tf_op jit(solution)/shard_map/ppermute | solution.py:145
  162.4 0.1 copy.37
  162.5 3.9 %collective-permute-done.6 = f32[128,128]{1,0:T(8,128)S(1)} collective-permute-done((f32[128,128]{1,0:T(8,128)S(1)}, f32[128,128]{1,0:T(8,128)S(1)}, u32[]{:S(2)}, u32[]{:S(2)}) %collective-permute-start.6) | collective-permute-done | bytes 65568 | tf_op jit(solution)/shard_map/ppermute | solution.py:145
  166.4 0.1 collective-permute-start.7
  166.6 0.7 copy.34
  167.3 3.5 %collective-permute-done.7 = f32[128,128]{1,0:T(8,128)S(1)} collective-permute-done((f32[128,128]{1,0:T(8,128)S(1)}, f32[128,128]{1,0:T(8,128)S(1)}, u32[]{:S(2)}, u32[]{:S(2)}) %collective-permute-start.7) | collective-permute-done | bytes 65568 | tf_op jit(solution)/shard_map/ppermute | solution.py:145
  170.8 0.7 copy.35
  (23 shorter events, 0.2 us)
Async XLA Ops:
  0.6 11.1 %copy-start = (s32[120,4]{0,1:T(4,128)S(1)}, s32[120,4]{0,1:T(4,128)}, u32[]{:S(2)}) copy-start(s32[120,4]{0,1:T(4,128)} %param.10) | copy-start | bytes 5764
  3.5 23.3 %all-to-all-start = ((bf16[16,256,128]{1,2,0:T(8,128)(2,1)}), bf16[16,256,128]{1,2,0:T(8,128)(2,1)S(1)}, u32[]{:S(2)}, u32[]{:S(2)}) async-start(bf16[16,256,128]{1,2,0:T(8,128)(2,1)} %broadcast_in_dim.10), calls=%async_computation | async-start | bytes 2097152 | tf_op jit(solution)/shard_map/all_to_all | solution.py:119
  12.6 7.4 %copy-start.3 = (s32[120]{0:T(128)S(1)}, s32[120]{0:T(128)}, u32[]{:S(2)}) copy-start(s32[120]{0:T(128)} %users_ref.3) | copy-start | bytes 1444
  12.6 7.5 %copy-start.4 = (s32[120]{0:T(128)S(1)}, s32[120]{0:T(128)}, u32[]{:S(2)}) copy-start(s32[120]{0:T(128)} %items_ref.3) | copy-start | bytes 1444
  35.5 39.7 %copy-start.1 = (f32[128,128]{1,0:T(8,128)S(1)}, f32[128,128]{1,0:T(8,128)}, u32[]{:S(2)}) copy-start(f32[128,128]{1,0:T(8,128)} %param.15) | copy-start | bytes 196612
  35.5 39.8 %copy-start.2 = (f32[128,128]{1,0:T(8,128)S(1)}, f32[128,128]{1,0:T(8,128)}, u32[]{:S(2)}) copy-start(f32[128,128]{1,0:T(8,128)} %param.14) | copy-start | bytes 196612
  71.0 1.3 collective-permute-start
  72.3 5.3 %collective-permute-start.1 = (f32[136,128]{1,0:T(8,128)S(1)}, f32[136,128]{1,0:T(8,128)S(1)}, u32[]{:S(2)}, u32[]{:S(2)}) collective-permute-start(f32[136,128]{1,0:T(8,128)S(1)} %slice_add_fusion.3), channel_id=1, source_target_pairs={{0,64},{16,80},{32,96},{48,112},{64,0},{80,16},{96,32},{112,48},{1... | collective-permute-start | bytes 208904 | tf_op jit(solution)/shard_map/ppermute | solution.py:145
  77.6 8.2 %collective-permute-start.2 = (f32[136,128]{1,0:T(8,128)S(1)}, f32[136,128]{1,0:T(8,128)S(1)}, u32[]{:S(2)}, u32[]{:S(2)}) collective-permute-start(f32[136,128]{1,0:T(8,128)S(1)} %add.94), channel_id=1, source_target_pairs={{0,192},{16,208},{32,224},{48,240},{64,128},{80,144},{96,160},{112... | collective-permute-start | bytes 208904 | tf_op jit(solution)/shard_map/ppermute | solution.py:145
  85.9 4.4 %collective-permute-start.3 = (f32[136,128]{1,0:T(8,128)S(1)}, f32[136,128]{1,0:T(8,128)S(1)}, u32[]{:S(2)}, u32[]{:S(2)}) collective-permute-start(f32[136,128]{1,0:T(8,128)S(1)} %add.95), channel_id=1, source_target_pairs={{0,32},{16,48},{32,0},{48,16},{64,96},{80,112},{96,64},{112,80},{1... | collective-permute-start | bytes 208904 | tf_op jit(solution)/shard_map/ppermute | solution.py:145
  149.0 1.3 collective-permute-start.4
  150.4 9.6 %collective-permute-start.5 = (f32[128,128]{1,0:T(8,128)S(1)}, f32[128,128]{1,0:T(8,128)S(1)}, u32[]{:S(2)}, u32[]{:S(2)}) collective-permute-start(f32[128,128]{1,0:T(8,128)S(1)} %get-tuple-element.11), channel_id=1, source_target_pairs={{0,64},{16,80},{32,96},{48,112},{64,0},{80,16},{96,32},{112,48},{1... | collective-permute-start | bytes 196616 | tf_op jit(solution)/shard_map/ppermute | solution.py:145
  159.9 6.5 %collective-permute-start.6 = (f32[128,128]{1,0:T(8,128)S(1)}, f32[128,128]{1,0:T(8,128)S(1)}, u32[]{:S(2)}, u32[]{:S(2)}) collective-permute-start(f32[128,128]{1,0:T(8,128)S(1)} %add.102), channel_id=1, source_target_pairs={{0,192},{16,208},{32,224},{48,240},{64,128},{80,144},{96,160},{112... | collective-permute-start | bytes 196616 | tf_op jit(solution)/shard_map/ppermute | solution.py:145
  166.4 4.4 %collective-permute-start.7 = (f32[128,128]{1,0:T(8,128)S(1)}, f32[128,128]{1,0:T(8,128)S(1)}, u32[]{:S(2)}, u32[]{:S(2)}) collective-permute-start(f32[128,128]{1,0:T(8,128)S(1)} %add.103), channel_id=1, source_target_pairs={{0,32},{16,48},{32,0},{48,16},{64,96},{80,112},{96,64},{112,80},{1... | collective-permute-start | bytes 196616 | tf_op jit(solution)/shard_map/ppermute | solution.py:145

commit v7 on v6

--- a/solution.py
+++ b/solution.py
@@ -18,9 +18,9 @@
 
 def tile_kernel(with_diag, per_block, count_ref, users_ref, items_ref, *refs):
     if with_diag:
-        panel_ref, ratings_ref, weighted_ref, diag_ref, acc_ref, residual_ref = refs
+        panel_ref, flip_ref, ratings_ref, weighted_ref, diag_ref, acc_ref, residual_ref = refs
     else:
-        panel_ref, ratings_ref, weighted_ref, acc_ref, residual_ref = refs
+        panel_ref, flip_ref, ratings_ref, weighted_ref, acc_ref, residual_ref = refs
     step = pl.program_id(0)
     side = ratings_ref.shape[1]
     f32, bf16 = jnp.float32, jnp.bfloat16
@@ -40,7 +40,7 @@
             ub = users_ref[slot]
             ib = items_ref[slot]
             user_rows = panel_ref[ub, 0:side, :]
-            item_cols = panel_ref[ib, 3 * side:4 * side, :]
+            item_cols = flip_ref[ib, :, side:2 * side]
             predicted = jnp.dot(user_rows, item_cols, preferred_element_type=f32)
             residual_ref[k] = (weighted_ref[k].astype(f32) * (ratings_ref[k].astype(f32) - predicted)).astype(bf16)
         for k in range(per_block):
@@ -49,12 +49,12 @@
             ib = items_ref[slot]
             residual = residual_ref[k]
             item_rows = panel_ref[ib, side:2 * side, :]
-            user_cols = panel_ref[ub, 2 * side:3 * side, :]
+            user_cols = flip_ref[ub, :, 0:side]
             acc_ref[ub, 0:side, :] += jnp.dot(residual, item_rows, preferred_element_type=f32)
             acc_ref[ib, side:2 * side, :] += jnp.dot(user_cols, residual, preferred_element_type=f32)
 
 
-def tile_terms(blocks, count, tile_users, tile_items, panel, ratings, weighted, diag=None):
+def tile_terms(blocks, count, tile_users, tile_items, panel, flip, ratings, weighted, diag=None):
     with_diag = diag is not None
     slots, side, _ = ratings.shape
     per_block = PER_BLOCK
@@ -70,15 +70,16 @@
 
     in_specs = [
         pl.BlockSpec(panel.shape, whole),
+        pl.BlockSpec(flip.shape, whole),
         pl.BlockSpec((per_block, side, side), tile_map),
         pl.BlockSpec((per_block, side, side), tile_map),
     ]
-    operands = [panel, ratings, weighted]
+    operands = [panel, flip, ratings, weighted]
     if with_diag:
         in_specs.append(pl.BlockSpec(diag.shape, whole))
         operands.append(diag)
     flops = slots * (3 * 2 * side * side * side)
-    bytes_accessed = 2 * ratings.size * 2 + panel.size * 2 + blocks * acc_rows * side * 4
+    bytes_accessed = 2 * ratings.size * 2 + 2 * panel.size * 2 + blocks * acc_rows * side * 4
     return pl.pallas_call(
         functools.partial(tile_kernel, with_diag, per_block),
         out_shape=jax.ShapeDtypeStruct((blocks, acc_rows, side), jnp.float32),
@@ -117,8 +118,7 @@
     own = jnp.concatenate([users.astype(jnp.bfloat16), items.astype(jnp.bfloat16)], axis=0)
     copies = jnp.broadcast_to(own[None], (blocks,) + own.shape)
     gathered = lax.all_to_all(copies, "item", 0, 0, tiled=False)
-    return jnp.concatenate([gathered, jnp.swapaxes(gathered[:, :users.shape[0]], 1, 2),
-                            jnp.swapaxes(gathered[:, users.shape[0]:], 1, 2)], axis=1)
+    return gathered, jnp.swapaxes(gathered, 1, 2)
 
 
 def user_rounds(groups):
@@ -153,8 +153,8 @@
     item_weight = None
     for iteration in range(STEPS):
         with_diag = iteration == 0
-        panel = gather_panel(users, items, blocks)
-        acc = tile_terms(blocks, tile_counts, tile_users, tile_items, panel, ratings, weighted,
+        panel, flip = gather_panel(users, items, blocks)
+        acc = tile_terms(blocks, tile_counts, tile_users, tile_items, panel, flip, ratings, weighted,
                          diag if with_diag else None)
         total = jnp.sum(lax.all_to_all(acc, "item", 0, 0, tiled=False), axis=0)
         item_total = sum_over_user(total[side:], groups)

time: 172 us -> 167 us (0.971)
  starting transfers between devices: 28 us -> 24.8 us
  other arithmetic: 13.3 us -> 10.3 us
    ppermute x8, starting transfers between devices: 20.5 us -> 17.3 us  [sum_over_user(): part = part + lax.ppermute(part, 'user', pairs)]
    concatenate x2 -> x0, other arithmetic: 2.98 us -> none  [gather_panel(): jnp.concatenate([gathered, jnp.swapaxes(gathered[:, :users.shape[0]], 1,...]
where the time goes in v7:
time: 167 us; the launch traced here: 166 us
  blocking collectives  83.8 us (50%)
  waiting for transfers between devices  26.5 us (16%)
  starting transfers between devices  24.8 us (15%)
  Pallas kernels  12.3 us (7%)
  other arithmetic  10.3 us (6%)
  local copies, waits for them, and re-layouts  6.58 us (4%)
    all_to_all x2, blocking collectives, on_device(): total = jnp.sum(lax.all_to_all(acc, 'item', 0, 0, tiled=False), axis=0)  65.7 us
    ppermute x8, waiting for transfers between devices, sum_over_user(): part = part + lax.ppermute(part, 'user', pairs)  20.7 us
    all_to_all x1, blocking collectives, gather_panel(): gathered = lax.all_to_all(copies, 'item', 0, 0, tiled=False)  18.1 us
    ppermute x8, starting transfers between devices, sum_over_user(): part = part + lax.ppermute(part, 'user', pairs)  17.3 us
    pallas_call x2, Pallas kernels, tile_terms(): pl.pallas_call(functools.partial(tile_kernel, with_diag, per_block), out_...  12.3 us
    all_to_all x1, starting transfers between devices, gather_panel(): gathered = lax.all_to_all(copies, 'item', 0, 0, tiled=False)  7.48 us
    reduce_sum x1, other arithmetic, prepare(): row_sums = jnp.sum(weighted, axis=2)  7.38 us
    all_to_all x1, waiting for transfers between devices, gather_panel(): gathered = lax.all_to_all(copies, 'item', 0, 0, tiled=False)  5.77 us
  transfers between devices with their start and end apart: 9, of which 9 were waited for; matrix products, arithmetic and copies ran while one was open for 6% of the time, Pallas kernels for 0%

profile of v7, /device:TPU:2, one launch (start us, length us, event | category | flops | bytes accessed | tf_op | source)
XLA Modules:
  0.0 165.9 jit_solution(9603204002766138484)
XLA Ops:
  0.6 0.0 copy-start
  0.6 0.9 convert_element_type.34
  1.5 0.8 convert_element_type.35
  2.3 0.1 copy.24
  2.5 1.1 broadcast_in_dim.10
  3.5 7.5 %all-to-all-start = ((bf16[16,256,128]{1,2,0:T(8,128)(2,1)}), bf16[16,256,128]{1,2,0:T(8,128)(2,1)S(1)}, u32[]{:S(2)}, u32[]{:S(2)}) async-start(bf16[16,256,128]{1,2,0:T(8,128)(2,1)} %broadcast_in_dim.10), calls=%async_computation | async-start | bytes 2097152 | tf_op jit(solution)/shard_map/all_to_all | solution.py:120
  11.7 0.0 copy-done
  11.7 0.6 gather_fusion
  12.4 0.1 multiply_bitcast_fusion
  12.5 0.1 copy.25
  12.6 0.1 pad.4.clone
  12.6 0.0 copy-start.5
  12.6 0.0 copy-start.6
  12.6 7.4 %fusion.1 = (f32[120,128]{1,0:T(8,128)S(1)}, f32[120,128]{1,0:T(8,128)S(1)}, bf16[120,128,128]{2,1,0:T(8,128)(2,1)}) fusion(bf16[120,128,128]{2,1,0:T(8,128)(2,1)} %param.9, f32[120,128]{1,0:T(8,128)S(1)} %copy.25), kind=kLoop, calls=%fused_computation.3 | loop fusion | flops 9799680 | bytes 8048640 | tf_op jit(solution)/shard_map/reduce_sum | solution.py:106
  20.0 0.0 copy-done.5
  20.0 0.1 fusion.9
  20.2 0.0 copy-done.6
  20.2 0.2 fusion.10
  20.3 0.7 maximum_maximum_fusion.refs_4_
  21.0 5.8 %all-to-all-done = bf16[16,256,128]{1,2,0:T(8,128)(2,1)S(1)} async-done(((bf16[16,256,128]{1,2,0:T(8,128)(2,1)}), bf16[16,256,128]{1,2,0:T(8,128)(2,1)S(1)}, u32[]{:S(2)}, u32[]{:S(2)}) %all-to-all-start) | async-done | bytes 1048608 | tf_op jit(solution)/shard_map/all_to_all | solution.py:120
  26.8 0.0 copy-start.1
  26.8 1.3 copy.26.refs_0_
  28.1 0.0 copy-done.1
  28.1 6.2 %shard_map.95 = f32[16,264,128]{2,1,0:T(8,128)} custom-call(s32[1]{0:T(128)} %copy.38.count_ref, s32[120]{0:T(128)} %users_ref.3, s32[120]{0:T(128)} %items_ref.3, bf16[16,256,128]{2,1,0:T(8,128)(2,1)} %copy.26.refs_0_, bf16[16,128,256]{2,1,0:T(8,128)(2,1)} %bitcast.34, bf16[120,128,128]{2,1,0:T(8,128)(2,1)} %refs_2_.3, ...), custom_call_target="tpu_custom_call" | custom-call | flops 1509949440 | bytes 12124160 | tf_op jit(solution)/shard_map/pallas_call | solution.py:83
  34.3 0.0 copy-start.3
  34.3 0.0 copy-start.4
  34.3 35.1 %all_to_all.20 = f32[16,264,128]{2,1,0:T(8,128)S(1)} all-to-all(f32[16,264,128]{2,1,0:T(8,128)} %shard_map.95), channel_id=1, replica_groups=mesh['user'=16,'item'=16] {'item'}, dimensions={0} | all-to-all | bytes 4325376 | tf_op jit(solution)/shard_map/all_to_all | solution.py:159
  69.4 0.1 reduce_sum.38
  69.5 0.1 collective-permute-start
  69.6 1.2 collective-permute-done
  70.9 3.6 %collective-permute-start.1 = (f32[136,128]{1,0:T(8,128)S(1)}, f32[136,128]{1,0:T(8,128)S(1)}, u32[]{:S(2)}, u32[]{:S(2)}) collective-permute-start(f32[136,128]{1,0:T(8,128)S(1)} %slice_add_fusion.3), channel_id=1, source_target_pairs={{0,64},{16,80},{32,96},{48,112},{64,0},{80,16},{96,32},{112,48},{1... | collective-permute-start | bytes 208904 | tf_op jit(solution)/shard_map/ppermute | solution.py:145
  74.5 0.0 copy-done.3
  74.5 0.1 copy.31
  74.6 0.0 copy-done.4
  74.6 0.1 copy.29
  74.7 3.8 %collective-permute-done.1 = f32[136,128]{1,0:T(8,128)S(1)} collective-permute-done((f32[136,128]{1,0:T(8,128)S(1)}, f32[136,128]{1,0:T(8,128)S(1)}, u32[]{:S(2)}, u32[]{:S(2)}) %collective-permute-start.1) | collective-permute-done | bytes 69664 | tf_op jit(solution)/shard_map/ppermute | solution.py:145
  78.5 4.7 %collective-permute-start.2 = (f32[136,128]{1,0:T(8,128)S(1)}, f32[136,128]{1,0:T(8,128)S(1)}, u32[]{:S(2)}, u32[]{:S(2)}) collective-permute-start(f32[136,128]{1,0:T(8,128)S(1)} %add.94), channel_id=1, source_target_pairs={{0,192},{16,208},{32,224},{48,240},{64,128},{80,144},{96,160},{112... | collective-permute-start | bytes 208904 | tf_op jit(solution)/shard_map/ppermute | solution.py:145
  83.2 0.1 copy.36
  83.3 2.2 %collective-permute-done.2 = f32[136,128]{1,0:T(8,128)S(1)} collective-permute-done((f32[136,128]{1,0:T(8,128)S(1)}, f32[136,128]{1,0:T(8,128)S(1)}, u32[]{:S(2)}, u32[]{:S(2)}) %collective-permute-start.2) | collective-permute-done | bytes 69664 | tf_op jit(solution)/shard_map/ppermute | solution.py:145
  85.5 1.6 collective-permute-start.3
  87.1 2.8 %collective-permute-done.3 = f32[136,128]{1,0:T(8,128)S(1)} collective-permute-done((f32[136,128]{1,0:T(8,128)S(1)}, f32[136,128]{1,0:T(8,128)S(1)}, u32[]{:S(2)}, u32[]{:S(2)}) %collective-permute-start.3) | collective-permute-done | bytes 69664 | tf_op jit(solution)/shard_map/ppermute | solution.py:145
  90.0 0.1 broadcast_in_dim.14
  90.1 18.1 %all_to_all.21 = bf16[16,256,128]{1,2,0:T(8,128)(2,1)S(1)} all-to-all(bf16[16,256,128]{1,2,0:T(8,128)(2,1)S(1)} %broadcast_in_dim.14), channel_id=1, replica_groups=mesh['user'=16,'item'=16] {'item'}, dimensions={0} | all-to-all | bytes 2097152 | tf_op jit(solution)/shard_map/all_to_all | solution.py:120
  108.2 0.0 copy-start.2
  108.2 1.3 copy.32.refs_0_
  109.5 0.0 copy-done.2
  109.5 6.1 %shard_map.96 = f32[16,256,128]{2,1,0:T(8,128)} custom-call(s32[1]{0:T(128)} %copy.38.count_ref, s32[120]{0:T(128)} %users_ref.3, s32[120]{0:T(128)} %items_ref.3, bf16[16,256,128]{2,1,0:T(8,128)(2,1)} %copy.32.refs_0_, bf16[16,128,256]{2,1,0:T(8,128)(2,1)} %bitcast.35, bf16[120,128,128]{2,1,0:T(8,128)(2,1)} %refs_2_.3, ...), custom_call_target="tpu_custom_call" | custom-call | flops 1509949440 | bytes 12058624 | tf_op jit(solution)/shard_map/pallas_call | solution.py:83
  115.6 30.6 %all_to_all.22 = f32[16,256,128]{2,1,0:T(8,128)S(1)} all-to-all(f32[16,256,128]{2,1,0:T(8,128)} %shard_map.96), channel_id=1, replica_groups=mesh['user'=16,'item'=16] {'item'}, dimensions={0} | all-to-all | bytes 4194304 | tf_op jit(solution)/shard_map/all_to_all | solution.py:159
  146.2 0.1 reduce_sum.39
  146.3 0.1 collective-permute-start.4
  146.4 1.2 collective-permute-done.4
  147.7 0.9 collective-permute-start.5
  148.6 4.4 %collective-permute-done.5 = f32[128,128]{1,0:T(8,128)S(1)} collective-permute-done((f32[128,128]{1,0:T(8,128)S(1)}, f32[128,128]{1,0:T(8,128)S(1)}, u32[]{:S(2)}, u32[]{:S(2)}) %collective-permute-start.5) | collective-permute-done | bytes 65568 | tf_op jit(solution)/shard_map/ppermute | solution.py:145
  153.0 5.6 %collective-permute-start.6 = (f32[128,128]{1,0:T(8,128)S(1)}, f32[128,128]{1,0:T(8,128)S(1)}, u32[]{:S(2)}, u32[]{:S(2)}) collective-permute-start(f32[128,128]{1,0:T(8,128)S(1)} %add.102), channel_id=1, source_target_pairs={{0,192},{16,208},{32,224},{48,240},{64,128},{80,144},{96,160},{112... | collective-permute-start | bytes 196616 | tf_op jit(solution)/shard_map/ppermute | solution.py:145
  158.5 0.1 copy.37
  158.6 2.2 %collective-permute-done.6 = f32[128,128]{1,0:T(8,128)S(1)} collective-permute-done((f32[128,128]{1,0:T(8,128)S(1)}, f32[128,128]{1,0:T(8,128)S(1)}, u32[]{:S(2)}, u32[]{:S(2)}) %collective-permute-start.6) | collective-permute-done | bytes 65568 | tf_op jit(solution)/shard_map/ppermute | solution.py:145
  160.8 0.7 collective-permute-start.7
  161.5 0.7 copy.34
  162.3 2.9 %collective-permute-done.7 = f32[128,128]{1,0:T(8,128)S(1)} collective-permute-done((f32[128,128]{1,0:T(8,128)S(1)}, f32[128,128]{1,0:T(8,128)S(1)}, u32[]{:S(2)}, u32[]{:S(2)}) %collective-permute-start.7) | collective-permute-done | bytes 65568 | tf_op jit(solution)/shard_map/ppermute | solution.py:145
  165.2 0.7 copy.35
  (23 shorter events, 0.3 us)
Async XLA Ops:
  0.6 11.1 %copy-start = (s32[120,4]{0,1:T(4,128)S(1)}, s32[120,4]{0,1:T(4,128)}, u32[]{:S(2)}) copy-start(s32[120,4]{0,1:T(4,128)} %param.10) | copy-start | bytes 5764
  3.5 23.3 %all-to-all-start = ((bf16[16,256,128]{1,2,0:T(8,128)(2,1)}), bf16[16,256,128]{1,2,0:T(8,128)(2,1)S(1)}, u32[]{:S(2)}, u32[]{:S(2)}) async-start(bf16[16,256,128]{1,2,0:T(8,128)(2,1)} %broadcast_in_dim.10), calls=%async_computation | async-start | bytes 2097152 | tf_op jit(solution)/shard_map/all_to_all | solution.py:120
  12.6 7.4 %copy-start.5 = (s32[120]{0:T(128)S(1)}, s32[120]{0:T(128)}, u32[]{:S(2)}) copy-start(s32[120]{0:T(128)} %users_ref.3) | copy-start | bytes 1444
  12.6 7.5 %copy-start.6 = (s32[120]{0:T(128)S(1)}, s32[120]{0:T(128)}, u32[]{:S(2)}) copy-start(s32[120]{0:T(128)} %items_ref.3) | copy-start | bytes 1444
  26.8 1.3 copy-start.1
  34.3 40.2 %copy-start.3 = (f32[128,128]{1,0:T(8,128)S(1)}, f32[128,128]{1,0:T(8,128)}, u32[]{:S(2)}) copy-start(f32[128,128]{1,0:T(8,128)} %param.15) | copy-start | bytes 196612
  34.3 40.3 %copy-start.4 = (f32[128,128]{1,0:T(8,128)S(1)}, f32[128,128]{1,0:T(8,128)}, u32[]{:S(2)}) copy-start(f32[128,128]{1,0:T(8,128)} %param.14) | copy-start | bytes 196612
  69.5 1.3 collective-permute-start
  70.9 7.6 %collective-permute-start.1 = (f32[136,128]{1,0:T(8,128)S(1)}, f32[136,128]{1,0:T(8,128)S(1)}, u32[]{:S(2)}, u32[]{:S(2)}) collective-permute-start(f32[136,128]{1,0:T(8,128)S(1)} %slice_add_fusion.3), channel_id=1, source_target_pairs={{0,64},{16,80},{32,96},{48,112},{64,0},{80,16},{96,32},{112,48},{1... | collective-permute-start | bytes 208904 | tf_op jit(solution)/shard_map/ppermute | solution.py:145
  78.5 7.0 %collective-permute-start.2 = (f32[136,128]{1,0:T(8,128)S(1)}, f32[136,128]{1,0:T(8,128)S(1)}, u32[]{:S(2)}, u32[]{:S(2)}) collective-permute-start(f32[136,128]{1,0:T(8,128)S(1)} %add.94), channel_id=1, source_target_pairs={{0,192},{16,208},{32,224},{48,240},{64,128},{80,144},{96,160},{112... | collective-permute-start | bytes 208904 | tf_op jit(solution)/shard_map/ppermute | solution.py:145
  85.5 4.4 %collective-permute-start.3 = (f32[136,128]{1,0:T(8,128)S(1)}, f32[136,128]{1,0:T(8,128)S(1)}, u32[]{:S(2)}, u32[]{:S(2)}) collective-permute-start(f32[136,128]{1,0:T(8,128)S(1)} %add.95), channel_id=1, source_target_pairs={{0,32},{16,48},{32,0},{48,16},{64,96},{80,112},{96,64},{112,80},{1... | collective-permute-start | bytes 208904 | tf_op jit(solution)/shard_map/ppermute | solution.py:145
  108.2 1.3 copy-start.2
  146.3 1.3 collective-permute-start.4
  147.7 5.3 %collective-permute-start.5 = (f32[128,128]{1,0:T(8,128)S(1)}, f32[128,128]{1,0:T(8,128)S(1)}, u32[]{:S(2)}, u32[]{:S(2)}) collective-permute-start(f32[128,128]{1,0:T(8,128)S(1)} %get-tuple-element.7), channel_id=1, source_target_pairs={{0,64},{16,80},{32,96},{48,112},{64,0},{80,16},{96,32},{112,48},{1... | collective-permute-start | bytes 196616 | tf_op jit(solution)/shard_map/ppermute | solution.py:145
  153.0 7.8 %collective-permute-start.6 = (f32[128,128]{1,0:T(8,128)S(1)}, f32[128,128]{1,0:T(8,128)S(1)}, u32[]{:S(2)}, u32[]{:S(2)}) collective-permute-start(f32[128,128]{1,0:T(8,128)S(1)} %add.102), channel_id=1, source_target_pairs={{0,192},{16,208},{32,224},{48,240},{64,128},{80,144},{96,160},{112... | collective-permute-start | bytes 196616 | tf_op jit(solution)/shard_map/ppermute | solution.py:145
  160.8 4.4 %collective-permute-start.7 = (f32[128,128]{1,0:T(8,128)S(1)}, f32[128,128]{1,0:T(8,128)S(1)}, u32[]{:S(2)}, u32[]{:S(2)}) collective-permute-start(f32[128,128]{1,0:T(8,128)S(1)} %add.103), channel_id=1, source_target_pairs={{0,32},{16,48},{32,0},{48,16},{64,96},{80,112},{96,64},{112,80},{1... | collective-permute-start | bytes 196616 | tf_op jit(solution)/shard_map/ppermute | solution.py:145

commit v8 on v7

--- a/solution.py
+++ b/solution.py
@@ -13,7 +13,7 @@
 STEP_SCALE = 4.0
 DECAY_RATE = 0.02
 
-PER_BLOCK = 40
+PER_BLOCK = 60
 
 
 def tile_kernel(with_diag, per_block, count_ref, users_ref, items_ref, *refs):

time: 167 us -> 171 us (1.024)
  waiting for transfers between devices: 26.5 us -> 29.8 us
  Pallas kernels: 12.3 us -> 14.3 us
    ppermute x8, waiting for transfers between devices: 20.7 us -> 24 us  [sum_over_user(): part = part + lax.ppermute(part, 'user', pairs)]
    pallas_call x2, Pallas kernels: 12.3 us -> 14.3 us  [tile_terms(): pl.pallas_call(functools.partial(tile_kernel, with_diag, per_block), out_...]
where the time goes in v8:
time: 171 us; the launch traced here: 170 us
  blocking collectives  83.5 us (49%)
  waiting for transfers between devices  29.8 us (17%)
  starting transfers between devices  23.8 us (14%)
  Pallas kernels  14.3 us (8%)
  other arithmetic  10.3 us (6%)
  local copies, waits for them, and re-layouts  6.58 us (4%)
    all_to_all x2, blocking collectives, on_device(): total = jnp.sum(lax.all_to_all(acc, 'item', 0, 0, tiled=False), axis=0)  64 us
    ppermute x8, waiting for transfers between devices, sum_over_user(): part = part + lax.ppermute(part, 'user', pairs)  24 us
    all_to_all x1, blocking collectives, gather_panel(): gathered = lax.all_to_all(copies, 'item', 0, 0, tiled=False)  19.5 us
    ppermute x8, starting transfers between devices, sum_over_user(): part = part + lax.ppermute(part, 'user', pairs)  16.3 us
    pallas_call x2, Pallas kernels, tile_terms(): pl.pallas_call(functools.partial(tile_kernel, with_diag, per_block), out_...  14.3 us
    all_to_all x1, starting transfers between devices, gather_panel(): gathered = lax.all_to_all(copies, 'item', 0, 0, tiled=False)  7.48 us
    reduce_sum x1, other arithmetic, prepare(): row_sums = jnp.sum(weighted, axis=2)  7.38 us
    all_to_all x1, waiting for transfers between devices, gather_panel(): gathered = lax.all_to_all(copies, 'item', 0, 0, tiled=False)  5.77 us
  transfers between devices with their start and end apart: 9, of which 9 were waited for; matrix products, arithmetic and copies ran while one was open for 6% of the time, Pallas kernels for 0%

profile of v8, /device:TPU:2, one launch (start us, length us, event | category | flops | bytes accessed | tf_op | source)
XLA Modules:
  0.0 170.1 jit_solution(9195440344076309758)
XLA Ops:
  0.6 0.0 copy-start
  0.6 0.9 convert_element_type.34
  1.5 0.8 convert_element_type.35
  2.3 0.1 copy.24
  2.5 1.1 broadcast_in_dim.10
  3.5 7.5 %all-to-all-start = ((bf16[16,256,128]{1,2,0:T(8,128)(2,1)}), bf16[16,256,128]{1,2,0:T(8,128)(2,1)S(1)}, u32[]{:S(2)}, u32[]{:S(2)}) async-start(bf16[16,256,128]{1,2,0:T(8,128)(2,1)} %broadcast_in_dim.10), calls=%async_computation | async-start | bytes 2097152 | tf_op jit(solution)/shard_map/all_to_all | solution.py:120
  11.7 0.0 copy-done
  11.7 0.6 gather_fusion
  12.4 0.1 multiply_bitcast_fusion
  12.5 0.1 copy.25
  12.6 0.1 pad.4.clone
  12.6 0.0 copy-start.5
  12.6 0.0 copy-start.6
  12.6 7.4 %fusion.1 = (f32[120,128]{1,0:T(8,128)S(1)}, f32[120,128]{1,0:T(8,128)S(1)}, bf16[120,128,128]{2,1,0:T(8,128)(2,1)}) fusion(bf16[120,128,128]{2,1,0:T(8,128)(2,1)} %param.9, f32[120,128]{1,0:T(8,128)S(1)} %copy.25), kind=kLoop, calls=%fused_computation.3 | loop fusion | flops 9799680 | bytes 8048640 | tf_op jit(solution)/shard_map/reduce_sum | solution.py:106
  20.0 0.0 copy-done.5
  20.0 0.1 fusion.9
  20.2 0.0 copy-done.6
  20.2 0.2 fusion.10
  20.3 0.7 maximum_maximum_fusion.refs_4_
  21.0 5.8 %all-to-all-done = bf16[16,256,128]{1,2,0:T(8,128)(2,1)S(1)} async-done(((bf16[16,256,128]{1,2,0:T(8,128)(2,1)}), bf16[16,256,128]{1,2,0:T(8,128)(2,1)S(1)}, u32[]{:S(2)}, u32[]{:S(2)}) %all-to-all-start) | async-done | bytes 1048608 | tf_op jit(solution)/shard_map/all_to_all | solution.py:120
  26.8 0.0 copy-start.1
  26.8 1.3 copy.26.refs_0_
  28.1 0.0 copy-done.1
  28.1 7.2 %shard_map.95 = f32[16,264,128]{2,1,0:T(8,128)} custom-call(s32[1]{0:T(128)} %copy.38.count_ref, s32[120]{0:T(128)} %users_ref.3, s32[120]{0:T(128)} %items_ref.3, bf16[16,256,128]{2,1,0:T(8,128)(2,1)} %copy.26.refs_0_, bf16[16,128,256]{2,1,0:T(8,128)(2,1)} %bitcast.34, bf16[120,128,128]{2,1,0:T(8,128)(2,1)} %refs_2_.3, ...), custom_call_target="tpu_custom_call" | custom-call | flops 1509949440 | bytes 12124160 | tf_op jit(solution)/shard_map/pallas_call | solution.py:83
  35.3 0.0 copy-start.3
  35.3 0.0 copy-start.4
  35.3 32.9 %all_to_all.20 = f32[16,264,128]{2,1,0:T(8,128)S(1)} all-to-all(f32[16,264,128]{2,1,0:T(8,128)} %shard_map.95), channel_id=1, replica_groups=mesh['user'=16,'item'=16] {'item'}, dimensions={0} | all-to-all | bytes 4325376 | tf_op jit(solution)/shard_map/all_to_all | solution.py:159
  68.3 0.1 reduce_sum.38
  68.4 0.1 collective-permute-start
  68.5 1.2 collective-permute-done
  69.8 3.0 %collective-permute-start.1 = (f32[136,128]{1,0:T(8,128)S(1)}, f32[136,128]{1,0:T(8,128)S(1)}, u32[]{:S(2)}, u32[]{:S(2)}) collective-permute-start(f32[136,128]{1,0:T(8,128)S(1)} %slice_add_fusion.3), channel_id=1, source_target_pairs={{0,64},{16,80},{32,96},{48,112},{64,0},{80,16},{96,32},{112,48},{1... | collective-permute-start | bytes 208904 | tf_op jit(solution)/shard_map/ppermute | solution.py:145
  72.8 0.0 copy-done.3
  72.8 0.1 copy.31
  72.9 0.0 copy-done.4
  72.9 0.1 copy.29
  73.0 2.3 %collective-permute-done.1 = f32[136,128]{1,0:T(8,128)S(1)} collective-permute-done((f32[136,128]{1,0:T(8,128)S(1)}, f32[136,128]{1,0:T(8,128)S(1)}, u32[]{:S(2)}, u32[]{:S(2)}) %collective-permute-start.1) | collective-permute-done | bytes 69664 | tf_op jit(solution)/shard_map/ppermute | solution.py:145
  75.3 8.3 %collective-permute-start.2 = (f32[136,128]{1,0:T(8,128)S(1)}, f32[136,128]{1,0:T(8,128)S(1)}, u32[]{:S(2)}, u32[]{:S(2)}) collective-permute-start(f32[136,128]{1,0:T(8,128)S(1)} %add.94), channel_id=1, source_target_pairs={{0,192},{16,208},{32,224},{48,240},{64,128},{80,144},{96,160},{112... | collective-permute-start | bytes 208904 | tf_op jit(solution)/shard_map/ppermute | solution.py:145
  83.6 0.1 copy.36
  83.7 2.3 %collective-permute-done.2 = f32[136,128]{1,0:T(8,128)S(1)} collective-permute-done((f32[136,128]{1,0:T(8,128)S(1)}, f32[136,128]{1,0:T(8,128)S(1)}, u32[]{:S(2)}, u32[]{:S(2)}) %collective-permute-start.2) | collective-permute-done | bytes 69664 | tf_op jit(solution)/shard_map/ppermute | solution.py:145
  85.9 3.0 %collective-permute-start.3 = (f32[136,128]{1,0:T(8,128)S(1)}, f32[136,128]{1,0:T(8,128)S(1)}, u32[]{:S(2)}, u32[]{:S(2)}) collective-permute-start(f32[136,128]{1,0:T(8,128)S(1)} %add.95), channel_id=1, source_target_pairs={{0,32},{16,48},{32,0},{48,16},{64,96},{80,112},{96,64},{112,80},{1... | collective-permute-start | bytes 208904 | tf_op jit(solution)/shard_map/ppermute | solution.py:145
  88.9 2.3 %collective-permute-done.3 = f32[136,128]{1,0:T(8,128)S(1)} collective-permute-done((f32[136,128]{1,0:T(8,128)S(1)}, f32[136,128]{1,0:T(8,128)S(1)}, u32[]{:S(2)}, u32[]{:S(2)}) %collective-permute-start.3) | collective-permute-done | bytes 69664 | tf_op jit(solution)/shard_map/ppermute | solution.py:145
  91.3 0.1 broadcast_in_dim.14
  91.4 19.5 %all_to_all.21 = bf16[16,256,128]{1,2,0:T(8,128)(2,1)S(1)} all-to-all(bf16[16,256,128]{1,2,0:T(8,128)(2,1)S(1)} %broadcast_in_dim.14), channel_id=1, replica_groups=mesh['user'=16,'item'=16] {'item'}, dimensions={0} | all-to-all | bytes 2097152 | tf_op jit(solution)/shard_map/all_to_all | solution.py:120
  110.8 0.0 copy-start.2
  110.8 1.3 copy.32.refs_0_
  112.2 0.0 copy-done.2
  112.2 7.1 %shard_map.96 = f32[16,256,128]{2,1,0:T(8,128)} custom-call(s32[1]{0:T(128)} %copy.38.count_ref, s32[120]{0:T(128)} %users_ref.3, s32[120]{0:T(128)} %items_ref.3, bf16[16,256,128]{2,1,0:T(8,128)(2,1)} %copy.32.refs_0_, bf16[16,128,256]{2,1,0:T(8,128)(2,1)} %bitcast.35, bf16[120,128,128]{2,1,0:T(8,128)(2,1)} %refs_2_.3, ...), custom_call_target="tpu_custom_call" | custom-call | flops 1509949440 | bytes 12058624 | tf_op jit(solution)/shard_map/pallas_call | solution.py:83
  119.3 31.1 %all_to_all.22 = f32[16,256,128]{2,1,0:T(8,128)S(1)} all-to-all(f32[16,256,128]{2,1,0:T(8,128)} %shard_map.96), channel_id=1, replica_groups=mesh['user'=16,'item'=16] {'item'}, dimensions={0} | all-to-all | bytes 4194304 | tf_op jit(solution)/shard_map/all_to_all | solution.py:159
  150.4 0.1 reduce_sum.39
  150.5 0.1 collective-permute-start.4
  150.6 1.2 collective-permute-done.4
  151.9 1.4 collective-permute-start.5
  153.3 5.2 %collective-permute-done.5 = f32[128,128]{1,0:T(8,128)S(1)} collective-permute-done((f32[128,128]{1,0:T(8,128)S(1)}, f32[128,128]{1,0:T(8,128)S(1)}, u32[]{:S(2)}, u32[]{:S(2)}) %collective-permute-start.5) | collective-permute-done | bytes 65568 | tf_op jit(solution)/shard_map/ppermute | solution.py:145
  158.5 0.3 collective-permute-start.6
  158.8 0.1 copy.37
  158.9 6.1 %collective-permute-done.6 = f32[128,128]{1,0:T(8,128)S(1)} collective-permute-done((f32[128,128]{1,0:T(8,128)S(1)}, f32[128,128]{1,0:T(8,128)S(1)}, u32[]{:S(2)}, u32[]{:S(2)}) %collective-permute-start.6) | collective-permute-done | bytes 65568 | tf_op jit(solution)/shard_map/ppermute | solution.py:145
  165.0 0.2 collective-permute-start.7
  165.2 0.7 copy.34
  166.0 3.4 %collective-permute-done.7 = f32[128,128]{1,0:T(8,128)S(1)} collective-permute-done((f32[128,128]{1,0:T(8,128)S(1)}, f32[128,128]{1,0:T(8,128)S(1)}, u32[]{:S(2)}, u32[]{:S(2)}) %collective-permute-start.7) | collective-permute-done | bytes 65568 | tf_op jit(solution)/shard_map/ppermute | solution.py:145
  169.4 0.7 copy.35
  (23 shorter events, 0.3 us)
Async XLA Ops:
  0.6 11.1 %copy-start = (s32[120,4]{0,1:T(4,128)S(1)}, s32[120,4]{0,1:T(4,128)}, u32[]{:S(2)}) copy-start(s32[120,4]{0,1:T(4,128)} %param.10) | copy-start | bytes 5764
  3.5 23.3 %all-to-all-start = ((bf16[16,256,128]{1,2,0:T(8,128)(2,1)}), bf16[16,256,128]{1,2,0:T(8,128)(2,1)S(1)}, u32[]{:S(2)}, u32[]{:S(2)}) async-start(bf16[16,256,128]{1,2,0:T(8,128)(2,1)} %broadcast_in_dim.10), calls=%async_computation | async-start | bytes 2097152 | tf_op jit(solution)/shard_map/all_to_all | solution.py:120
  12.6 7.4 %copy-start.5 = (s32[120]{0:T(128)S(1)}, s32[120]{0:T(128)}, u32[]{:S(2)}) copy-start(s32[120]{0:T(128)} %users_ref.3) | copy-start | bytes 1444
  12.6 7.5 %copy-start.6 = (s32[120]{0:T(128)S(1)}, s32[120]{0:T(128)}, u32[]{:S(2)}) copy-start(s32[120]{0:T(128)} %items_ref.3) | copy-start | bytes 1444
  26.8 1.3 copy-start.1
  35.3 37.5 %copy-start.3 = (f32[128,128]{1,0:T(8,128)S(1)}, f32[128,128]{1,0:T(8,128)}, u32[]{:S(2)}) copy-start(f32[128,128]{1,0:T(8,128)} %param.15) | copy-start | bytes 196612
  35.3 37.6 %copy-start.4 = (f32[128,128]{1,0:T(8,128)S(1)}, f32[128,128]{1,0:T(8,128)}, u32[]{:S(2)}) copy-start(f32[128,128]{1,0:T(8,128)} %param.14) | copy-start | bytes 196612
  68.4 1.3 collective-permute-start
  69.8 5.5 %collective-permute-start.1 = (f32[136,128]{1,0:T(8,128)S(1)}, f32[136,128]{1,0:T(8,128)S(1)}, u32[]{:S(2)}, u32[]{:S(2)}) collective-permute-start(f32[136,128]{1,0:T(8,128)S(1)} %slice_add_fusion.3), channel_id=1, source_target_pairs={{0,64},{16,80},{32,96},{48,112},{64,0},{80,16},{96,32},{112,48},{1... | collective-permute-start | bytes 208904 | tf_op jit(solution)/shard_map/ppermute | solution.py:145
  75.3 10.6 %collective-permute-start.2 = (f32[136,128]{1,0:T(8,128)S(1)}, f32[136,128]{1,0:T(8,128)S(1)}, u32[]{:S(2)}, u32[]{:S(2)}) collective-permute-start(f32[136,128]{1,0:T(8,128)S(1)} %add.94), channel_id=1, source_target_pairs={{0,192},{16,208},{32,224},{48,240},{64,128},{80,144},{96,160},{112... | collective-permute-start | bytes 208904 | tf_op jit(solution)/shard_map/ppermute | solution.py:145
  85.9 5.3 %collective-permute-start.3 = (f32[136,128]{1,0:T(8,128)S(1)}, f32[136,128]{1,0:T(8,128)S(1)}, u32[]{:S(2)}, u32[]{:S(2)}) collective-permute-start(f32[136,128]{1,0:T(8,128)S(1)} %add.95), channel_id=1, source_target_pairs={{0,32},{16,48},{32,0},{48,16},{64,96},{80,112},{96,64},{112,80},{1... | collective-permute-start | bytes 208904 | tf_op jit(solution)/shard_map/ppermute | solution.py:145
  110.8 1.3 copy-start.2
  150.5 1.3 collective-permute-start.4
  151.9 6.7 %collective-permute-start.5 = (f32[128,128]{1,0:T(8,128)S(1)}, f32[128,128]{1,0:T(8,128)S(1)}, u32[]{:S(2)}, u32[]{:S(2)}) collective-permute-start(f32[128,128]{1,0:T(8,128)S(1)} %get-tuple-element.7), channel_id=1, source_target_pairs={{0,64},{16,80},{32,96},{48,112},{64,0},{80,16},{96,32},{112,48},{1... | collective-permute-start | bytes 196616 | tf_op jit(solution)/shard_map/ppermute | solution.py:145
  158.5 6.5 %collective-permute-start.6 = (f32[128,128]{1,0:T(8,128)S(1)}, f32[128,128]{1,0:T(8,128)S(1)}, u32[]{:S(2)}, u32[]{:S(2)}) collective-permute-start(f32[128,128]{1,0:T(8,128)S(1)} %add.102), channel_id=1, source_target_pairs={{0,192},{16,208},{32,224},{48,240},{64,128},{80,144},{96,160},{112... | collective-permute-start | bytes 196616 | tf_op jit(solution)/shard_map/ppermute | solution.py:145
  165.0 4.4 %collective-permute-start.7 = (f32[128,128]{1,0:T(8,128)S(1)}, f32[128,128]{1,0:T(8,128)S(1)}, u32[]{:S(2)}, u32[]{:S(2)}) collective-permute-start(f32[128,128]{1,0:T(8,128)S(1)} %add.103), channel_id=1, source_target_pairs={{0,32},{16,48},{32,0},{48,16},{64,96},{80,112},{96,64},{112,80},{1... | collective-permute-start | bytes 196616 | tf_op jit(solution)/shard_map/ppermute | solution.py:145
